TPU v7x, 512 devices: a whole 4x8x8 slice. The times are simulated.
512 devices in a mesh: dp: 8 (over z), expert: 64 (over y, x, core).
Axes of the slice: x: 4, y: 8, z: 8, core: 2. Of those that a mesh axis runs over, the one named last changes fastest.
Arguments:
- query: bfloat16 [128, 8192], P('dp'), may hold values from -1200 to 1200
- new_kv: bfloat16 [128, 1024], P('dp'), may hold values from -5 to 5
- kv_cache: bfloat16 [128, 1024, 1024], P('dp', 'expert'), may hold values from -6 to 6
- lengths: int32 [128], P('dp'), may hold values from 2 to 1024, as said below
- fork_parent: int32 [64], replicated, may hold values from 0 to 127, as said below
- fork_child: int32 [64], replicated, may hold values from 0 to 126, as said below
- fork_block: int32 [64], replicated, may hold values from 0 to 63, as said below
- out_weight: bfloat16 [8192, 4096], P('expert'), may hold values from -1 to 1
- residual: bfloat16 [128, 4096], P('dp'), may hold values from -300 to 300
- route_ids: int32 [128, 8], replicated, may hold values from 0 to 63, all different within a row; in each aligned block of 16 rows (0 to 15, 16 to 31, ...) at most 4 rows name the same one
- route_weights: float32 [128, 8], replicated, may hold values from 0.02 to 0.3
- w_gate: bfloat16 [64, 4096, 1024], P('expert', None, 'dp'), may hold values from -0.09375 to 0.09375
- w_up: bfloat16 [64, 4096, 1024], P('expert', None, 'dp'), may hold values from -0.09375 to 0.09375
- w_down: bfloat16 [64, 1024, 4096], P('expert', 'dp'), may hold values from -0.1875 to 0.1875
Outputs:
- attn_proj: bfloat16 [128, 4096], P('dp', 'expert')
- expert_mix: bfloat16 [128, 4096], P('dp', 'expert')
Inputs may be any that keep to these rules, and one draw needn't show every extreme that they name: `lengths`: at least 2; a fork's child has its parent's length. `fork_parent`: fork g * 8 + d takes its parent from the branches g * 16 to (g + 1) * 16 - 1 and its child from d * 16 to (d + 1) * 16 - 1; parents are distinct, children are distinct, and no child is a parent. `fork_child`: see fork_parent. `fork_block`: at most the block that holds the parent's last cached position, (lengths - 1) // 16. `route_ids`: in each aligned block of 16 rows no expert is named by more than 4 rows, a bound that some block reaches.
All inputs are finite; a program needn't handle non-finite values.
Results may differ from a plain program's by a relative error of at most 0.024.
Values may be sent and summed in bfloat16 or wider, within the bound.
No kernel may reach another device: no remote copies, remote signals or barrier semaphores. Data moves between devices by JAX's collectives and lax.ppermute only.
A program may use at most 128 MiB of HBM per device.

v0:
```python
import math

import jax
import jax.numpy as jnp
from jax import lax
from jax.sharding import PartitionSpec as P

HD = 128
KVH = 4


def combined_all(array, axis, join):
    gathered = jax.tree.map(
        lambda a, kind: lax.all_gather(a.astype(kind), axis),
        array,
        (jnp.bfloat16, jnp.bfloat16, jnp.bfloat16),
    )

    def take(source):
        return jax.tree.map(
            lambda a, own: lax.dynamic_index_in_dim(a, source, 0, False).astype(own.dtype),
            gathered,
            array,
        )

    return lax.fori_loop(
        1, lax.axis_size(axis), lambda source, state: join(state, take(source)), take(0)
    )


def combine_parts(first, second):
    out_first, peak_first, sum_first = first
    out_second, peak_second, sum_second = second
    highest = jnp.maximum(peak_first, peak_second)
    factor_first = jnp.exp(peak_first - highest)
    factor_second = jnp.exp(peak_second - highest)
    merged_out = out_first * factor_first[..., None] + out_second * factor_second[..., None]
    return (merged_out, highest, sum_first * factor_first + sum_second * factor_second)


def shards(
    query,
    new_kv,
    kv_cache,
    lengths,
    fork_parent,
    fork_child,
    fork_block,
    out_weight,
    residual,
    route_ids,
    route_weights,
    w_gate,
    w_up,
    w_down,
):
    groups = lax.axis_size("dp")
    owners = lax.axis_size("expert")
    group_index = lax.axis_index("dp")
    owner_index = lax.axis_index("expert")
    local_rows = query.shape[0]
    positions_dev = kv_cache.shape[1]
    key_width = KVH * HD
    head_count = query.shape[1] // HD
    grouping = head_count // KVH
    own_heads = head_count // owners
    model_width = residual.shape[1]
    columns = model_width // owners
    outgoing = (
        lax.dynamic_slice_in_dim(fork_parent, group_index * groups, groups)
        - group_index * local_rows
    )
    out_blocks = lax.dynamic_slice_in_dim(fork_block, group_index * groups, groups)
    send_rows = jnp.where(
        (owner_index >= out_blocks)[:, None, None],
        kv_cache[outgoing],
        jnp.zeros((), kv_cache.dtype),
    )
    arrived = lax.all_to_all(send_rows, "dp", split_axis=0, concat_axis=0, tiled=True)
    incoming = jnp.arange(groups, dtype=jnp.int32) * groups + group_index
    targets = fork_child[incoming] - group_index * local_rows
    take_new = owner_index >= fork_block[incoming]
    cache = kv_cache.at[targets].set(jnp.where(take_new[:, None, None], arrived, kv_cache[targets]))
    score_scale = 1.0 / math.sqrt(HD)
    positions = owner_index * positions_dev + jnp.arange(positions_dev, dtype=jnp.int32)
    visible = positions[None, :] < lengths[:, None]
    cached_keys = cache[:, :, :key_width].reshape(local_rows, positions_dev, KVH, HD)
    cached_values = cache[:, :, key_width:].reshape(local_rows, positions_dev, KVH, HD)
    grouped = query.reshape(local_rows, KVH, grouping, HD)
    scores = (
        jnp.einsum("bkgd,bpkd->bkgp", grouped, cached_keys, preferred_element_type=jnp.float32)
        * score_scale
    )
    scores = jnp.where(visible[:, None, None, :], scores, -1e30)
    highest = jnp.max(scores, axis=3)
    weights = jnp.where(visible[:, None, None, :], jnp.exp(scores - highest[..., None]), 0.0)
    weight_sum = jnp.sum(weights, axis=3)
    partial_out = jnp.einsum(
        "bkgp,bpkd->bkgd",
        weights.astype(jnp.bfloat16),
        cached_values,
        preferred_element_type=jnp.float32,
    )
    partial_out = partial_out.reshape(local_rows, head_count, HD)
    highest = highest.reshape(local_rows, head_count)
    weight_sum = weight_sum.reshape(local_rows, head_count)
    merged = combined_all((partial_out, highest, weight_sum), "expert", combine_parts)
    head_out = lax.dynamic_slice_in_dim(merged[0], owner_index * own_heads, own_heads, 1)
    head_peak = lax.dynamic_slice_in_dim(merged[1], owner_index * own_heads, own_heads, 1)
    head_sum = lax.dynamic_slice_in_dim(merged[2], owner_index * own_heads, own_heads, 1)
    own_query = lax.dynamic_slice_in_dim(query, owner_index * own_heads * HD, own_heads * HD, 1)
    own_query = own_query.reshape(local_rows, own_heads, HD).astype(jnp.float32)
    kv_index = (owner_index * own_heads + jnp.arange(own_heads, dtype=jnp.int32)) // grouping
    new_keys = jnp.take(
        new_kv[:, :key_width].reshape(local_rows, KVH, HD), kv_index, axis=1
    ).astype(jnp.float32)
    new_values = jnp.take(
        new_kv[:, key_width:].reshape(local_rows, KVH, HD), kv_index, axis=1
    ).astype(jnp.float32)
    own_score = jnp.sum(own_query * new_keys, axis=2) * score_scale
    new_peak = jnp.maximum(head_peak, own_score)
    old_factor = jnp.exp(head_peak - new_peak)
    own_weight = jnp.exp(own_score - new_peak)
    denominator = head_sum * old_factor + own_weight
    own_rounded = lax.optimization_barrier(own_weight.astype(jnp.bfloat16)).astype(jnp.float32)
    attended = (
        head_out * old_factor[..., None] + own_rounded[..., None] * new_values
    ) / denominator[..., None]
    attended = attended.astype(jnp.bfloat16).reshape(local_rows, own_heads * HD)
    proj_terms = jnp.dot(attended, out_weight, preferred_element_type=jnp.float32)
    projected = lax.psum(proj_terms, "expert")
    stream = residual.astype(jnp.float32) + projected
    inverse = lax.rsqrt(jnp.sum(stream * stream, axis=1, keepdims=True) / model_width + 1e-06)
    normed = (stream * inverse).astype(jnp.bfloat16)
    attn_cols = lax.dynamic_slice_in_dim(projected, owner_index * columns, columns, 1).astype(
        jnp.bfloat16
    )
    top_k = route_ids.shape[1]
    experts_total = w_gate.shape[0] * owners
    capacity = max(2, 2 * local_rows * top_k // experts_total)
    own_ids = lax.dynamic_slice_in_dim(route_ids, group_index * local_rows, local_rows, 0)
    own_gates = lax.dynamic_slice_in_dim(route_weights, group_index * local_rows, local_rows, 0)
    matched = (own_ids == owner_index).astype(jnp.int32).reshape(-1)
    ranking = jnp.cumsum(matched) - 1
    slot_ids = jnp.arange(capacity, dtype=jnp.int32)
    onehot = ((matched[:, None] == 1) & (ranking[:, None] == slot_ids[None, :])).astype(jnp.float32)
    chosen = onehot.reshape(local_rows, top_k, capacity)
    dispatch = jnp.sum(chosen, axis=1).T
    slot_gate = jnp.sum(chosen * own_gates[:, :, None], axis=(0, 1))
    dispatch, slot_gate = (dispatch, slot_gate)
    routed = jnp.dot(
        dispatch.astype(jnp.bfloat16), normed, preferred_element_type=jnp.float32
    ).astype(jnp.bfloat16)
    piece = lax.all_gather(routed, "dp", axis=0, tiled=True)
    gate_proj = jnp.dot(piece, w_gate[0], preferred_element_type=jnp.float32)
    up_proj = jnp.dot(piece, w_up[0], preferred_element_type=jnp.float32)
    hidden = (jax.nn.silu(gate_proj) * up_proj).astype(jnp.bfloat16)
    outputs = jnp.dot(hidden, w_down[0], preferred_element_type=jnp.float32)
    summed = lax.psum_scatter(
        outputs.astype(jnp.bfloat16), "dp", scatter_dimension=0, tiled=True
    ).astype(jnp.float32)
    spread = jnp.dot(dispatch.T * slot_gate[None, :], summed, precision=lax.Precision.HIGHEST)
    mix_cols = lax.psum_scatter(spread, "expert", scatter_dimension=1, tiled=True).astype(
        jnp.bfloat16
    )
    return (attn_cols, mix_cols)


def solution(mesh):
    in_specs = (
        P("dp", None),
        P("dp", None),
        P("dp", "expert", None),
        P("dp"),
        P(),
        P(),
        P(),
        P("expert", None),
        P("dp", None),
        P(),
        P(),
        P("expert", None, "dp"),
        P("expert", None, "dp"),
        P("expert", "dp", None),
    )
    out_specs = (P("dp", "expert"), P("dp", "expert"))
    return jax.shard_map(shards, mesh=mesh, in_specs=in_specs, out_specs=out_specs, check_vma=False)
```

profile of v0, /device:TPU:1, one launch (start us, length us, event | category | flops | bytes accessed | tf_op | source)
XLA Modules:
  0.0 683.1 jit_solution(2898068980157066316)
XLA Ops:
  11.2 10.9 %all-to-all-start = ((bf16[8,16,1024]{2,1,0:T(8,128)(2,1)}), bf16[8,16,1024]{2,1,0:T(8,128)(2,1)S(1)}, u32[]{:S(2)}, u32[]{:S(2)}) async-start(bf16[8,16,1024]{2,1,0:T(8,128)(2,1)} %broadcast_select_fusion), calls=%async_computation | async-start | bytes 524288 | tf_op jit(solution)/shard_map/all_to_all | solution.py:79
  25.4 1.7 copy.82
  27.8 4.7 all-to-all-done
  39.1 42.4 %all_gather.17 = bf16[64,16,64]{2,1,0:T(8,128)(2,1)S(1)} all-gather(bf16[1,16,64]{2,1,0:T(8,128)(2,1)S(1)} %convert_element_type.161), channel_id=1, replica_groups=mesh['dp'=8,'expert'=64] {'expert'}, dimensions={0}, use_global_device_ids=true | all-gather | bytes 133120 | tf_op jit(solution)/shard_map/all_gather | solution.py:14
  81.5 37.3 %all_gather.16 = bf16[64,16,64]{2,1,0:T(8,128)(2,1)S(1)} all-gather(bf16[1,16,64]{2,1,0:T(8,128)(2,1)S(1)} %convert_element_type.157), channel_id=1, replica_groups=mesh['dp'=8,'expert'=64] {'expert'}, dimensions={0}, use_global_device_ids=true | all-gather | bytes 133120 | tf_op jit(solution)/shard_map/all_gather | solution.py:14
  118.7 21.4 %all-gather.3.cloned.1.call-done = bf16[64,16,64,128]{3,2,1,0:T(8,128)(2,1)} async-done(((bf16[1,16,64,128]{3,2,1,0:T(8,128)(2,1)}), bf16[64,16,64,128]{3,2,1,0:T(8,128)(2,1)}) %all-gather.3.cloned.1.call-update) | async-done | bytes 16777232 | tf_op jit(solution)/shard_map/all_gather | solution.py:14
  141.2 94.9 %while.20 = (s32[]{:T(128)}, f32[16,64,128]{2,1,0:T(8,128)S(1)}, f32[16,64]{1,0:T(8,128)S(1)}, f32[16,64]{1,0:T(8,128)S(1)}, bf16[64,16,64]{2,1,0:T(8,128)(2,1)S...) while((s32[]{:T(128)}, f32[16,64,128]{2,1,0:T(8,128)S(1)}, ...), condition=%wide.region_4.5_spmd, body=%wide.region_3.4_spmd.sunk | while | flops 532485 | bytes 1347735 | solution.py:26
  141.2 1.5 fusion.71
  144.2 1.5 fusion.71
  147.2 1.5 fusion.71
  150.2 1.5 fusion.71
  153.3 1.5 fusion.71
  156.3 1.5 fusion.71
  159.3 1.5 fusion.71
  160.8 1.5 fusion.71
  162.3 1.5 fusion.71
  163.8 1.5 fusion.71
  238.0 183.2 %all-reduce.4.cloned.1.call-done = f32[16,4096]{1,0:T(8,128)} async-done(((f32[16,4096]{1,0:T(8,128)}), f32[16,4096]{1,0:T(8,128)}) %all-reduce.4.cloned.1.call-update) | async-done | bytes 262160 | tf_op jit(solution)/shard_map/psum | solution.py:131
  423.5 20.5 %all-gather = bf16[8,4,4096]{2,1,0:T(4,128)(2,1)S(1)} all-gather(bf16[1,4,4096]{2,1,0:T(4,128)(2,1)S(1)} %fusion.3), channel_id=1, replica_groups=mesh['dp'=8,'expert'=64] {'dp'}, dimensions={0}, use_global_device_ids=true | all-gather | bytes 294912 | tf_op jit(solution)/shard_map/all_gather | solution.py:154
  444.1 1.5 fusion.10
  445.6 2.5 convolution_convert_fusion
  450.1 74.1 %all-reduce.6.cloned.1.call-done = bf16[32,4096]{1,0:T(8,128)(2,1)} async-done(((bf16[32,4096]{1,0:T(8,128)(2,1)}), bf16[32,4096]{1,0:T(8,128)(2,1)}) %all-reduce.6.cloned.1.call-update) | async-done | bytes 262160
  524.2 3.4 convolution_bitcast_fusion
  529.0 146.2 %reduce-scatter.4.cloned.1.call-done = f32[64,16]{1,0:T(8,128)} async-done(((f32[4096,16]{1,0:T(8,128)}), f32[64,16]{1,0:T(8,128)}) %reduce-scatter.4.cloned.1.call-update) | async-done | bytes 4112
  (188 shorter events, 102.2 us)
Async XLA Ops:
  7.2 438.4 %copy-start = (bf16[1,128,4096]{2,1,0:T(8,128)(2,1)S(1)}, bf16[1,128,4096]{2,1,0:T(8,128)(2,1)}, u32[]{:S(2)}) copy-start(bf16[1,128,4096]{2,1,0:T(8,128)(2,1)} %param.31) | copy-start | bytes 3145732
  7.2 229.4 %copy-start.1 = (bf16[128,4096]{1,0:T(8,128)(2,1)S(1)}, bf16[128,4096]{1,0:T(8,128)(2,1)}, u32[]{:S(2)}) copy-start(bf16[128,4096]{1,0:T(8,128)(2,1)} %param.25) | copy-start | bytes 3145732
  7.2 414.1 %copy-start.2 = (bf16[16,4096]{1,0:T(8,128)(2,1)S(1)}, bf16[16,4096]{1,0:T(8,128)(2,1)}, u32[]{:S(2)}) copy-start(bf16[16,4096]{1,0:T(8,128)(2,1)} %param.26) | copy-start | bytes 393220
  7.2 230.5 %copy-start.3 = (f32[128,8]{0,1:T(8,128)S(1)}, f32[128,8]{0,1:T(8,128)}, u32[]{:S(2)}) copy-start(f32[128,8]{0,1:T(8,128)} %param.28) | copy-start | bytes 12292
  11.2 21.2 %all-to-all-start = ((bf16[8,16,1024]{2,1,0:T(8,128)(2,1)}), bf16[8,16,1024]{2,1,0:T(8,128)(2,1)S(1)}, u32[]{:S(2)}, u32[]{:S(2)}) async-start(bf16[8,16,1024]{2,1,0:T(8,128)(2,1)} %broadcast_select_fusion), calls=%async_computation | async-start | bytes 524288 | tf_op jit(solution)/shard_map/all_to_all | solution.py:79
  22.1 118.1 %all-gather.3.cloned.1.call-start = ((), (), s32[]{:S(2)}) async-start(), calls=%async_computation.2 | async-start | bytes 17039360 | tf_op jit(solution)/shard_map/all_gather | solution.py:14
  35.8 385.5 %all-reduce.4.cloned.1.call-start = ((), (), s32[]{:S(2)}) async-start(), calls=%async_computation.3 | async-start | bytes 524288 | tf_op jit(solution)/shard_map/psum | solution.py:131
  237.6 286.5 %all-reduce.6.cloned.1.call-start = ((), (), s32[]{:S(2)}) async-start(), calls=%async_computation.5 | async-start | bytes 524288
  448.1 227.1 %reduce-scatter.4.cloned.1.call-start = ((), (), s32[]{:S(2)}) async-start(), calls=%async_computation.4 | async-start | bytes 2129920
Sparse Core Ops, SparseCore 0:
  35.9 104.2 all-gather.2
  237.7 183.4 all-reduce.3
  448.2 75.9 all-reduce.5
  528.6 146.4 reduce-scatter.3
where the time goes:
time: 690 us; the launch traced here: 683 us
  waiting for transfers between devices  430 us (62%)
  other arithmetic  100 us (14%)
  blocking collectives  100 us (14%)
  between operations  14.7 us (2%)
  local copies, waits for them, and re-layouts  13.4 us (2%)
  matrix products  11.9 us (2%)
  starting transfers between devices  11 us (2%)
    unnamed x6, waiting for transfers between devices  220 us
    psum x1, waiting for transfers between devices, shards(): projected = lax.psum(proj_terms, 'expert')  183 us
    add x63, other arithmetic, combine_parts(): out_first * factor_first[..., None] + out_second * factor_second[..., None]  91.5 us
    all_gather x2, blocking collectives, combined_all(): lax.all_gather(a.astype(kind), axis)  79.6 us
    all_gather x1, waiting for transfers between devices, combined_all(): lax.all_gather(a.astype(kind), axis)  21.4 us
    all_gather x1, blocking collectives, shards(): piece = lax.all_gather(routed, 'dp', axis=0, tiled=True)  20.5 us
  transfers between devices with their start and end apart: 5, of which 5 were waited for; matrix products, arithmetic and copies ran while one was open for 2% of the time, Pallas kernels for 0%

commit v1 on v0

--- a/solution.py
+++ b/solution.py
@@ -9,33 +9,14 @@
 KVH = 4
 
 
-def combined_all(array, axis, join):
-    gathered = jax.tree.map(
-        lambda a, kind: lax.all_gather(a.astype(kind), axis),
-        array,
-        (jnp.bfloat16, jnp.bfloat16, jnp.bfloat16),
-    )
-
-    def take(source):
-        return jax.tree.map(
-            lambda a, own: lax.dynamic_index_in_dim(a, source, 0, False).astype(own.dtype),
-            gathered,
-            array,
-        )
-
-    return lax.fori_loop(
-        1, lax.axis_size(axis), lambda source, state: join(state, take(source)), take(0)
-    )
+def spread_to_owners(blocks, axis):
+    return lax.all_to_all(blocks, axis, 0, 0, tiled=True)
 
 
-def combine_parts(first, second):
-    out_first, peak_first, sum_first = first
-    out_second, peak_second, sum_second = second
-    highest = jnp.maximum(peak_first, peak_second)
-    factor_first = jnp.exp(peak_first - highest)
-    factor_second = jnp.exp(peak_second - highest)
-    merged_out = out_first * factor_first[..., None] + out_second * factor_second[..., None]
-    return (merged_out, highest, sum_first * factor_first + sum_second * factor_second)
+def gather_from_all(block, axis):
+    count = lax.axis_size(axis)
+    stacked = jnp.broadcast_to(block[None], (count,) + block.shape)
+    return spread_to_owners(stacked, axis)
 
 
 def shards(
@@ -66,6 +47,7 @@
     own_heads = head_count // owners
     model_width = residual.shape[1]
     columns = model_width // owners
+
     outgoing = (
         lax.dynamic_slice_in_dim(fork_parent, group_index * groups, groups)
         - group_index * local_rows
@@ -81,6 +63,7 @@
     targets = fork_child[incoming] - group_index * local_rows
     take_new = owner_index >= fork_block[incoming]
     cache = kv_cache.at[targets].set(jnp.where(take_new[:, None, None], arrived, kv_cache[targets]))
+
     score_scale = 1.0 / math.sqrt(HD)
     positions = owner_index * positions_dev + jnp.arange(positions_dev, dtype=jnp.int32)
     visible = positions[None, :] < lengths[:, None]
@@ -101,13 +84,18 @@
         cached_values,
         preferred_element_type=jnp.float32,
     )
-    partial_out = partial_out.reshape(local_rows, head_count, HD)
-    highest = highest.reshape(local_rows, head_count)
-    weight_sum = weight_sum.reshape(local_rows, head_count)
-    merged = combined_all((partial_out, highest, weight_sum), "expert", combine_parts)
-    head_out = lax.dynamic_slice_in_dim(merged[0], owner_index * own_heads, own_heads, 1)
-    head_peak = lax.dynamic_slice_in_dim(merged[1], owner_index * own_heads, own_heads, 1)
-    head_sum = lax.dynamic_slice_in_dim(merged[2], owner_index * own_heads, own_heads, 1)
+
+    send_out = partial_out.reshape(local_rows, owners, own_heads, HD).transpose(1, 0, 2, 3)
+    send_peak = highest.reshape(local_rows, owners, own_heads).transpose(1, 0, 2)
+    send_sum = weight_sum.reshape(local_rows, owners, own_heads).transpose(1, 0, 2)
+    got_out = spread_to_owners(send_out.astype(jnp.bfloat16), "expert").astype(jnp.float32)
+    got_peak = spread_to_owners(send_peak, "expert")
+    got_sum = spread_to_owners(send_sum, "expert")
+    head_peak = jnp.max(got_peak, axis=0)
+    factors = jnp.exp(got_peak - head_peak[None])
+    head_out = jnp.sum(got_out * factors[..., None], axis=0)
+    head_sum = jnp.sum(got_sum * factors, axis=0)
+
     own_query = lax.dynamic_slice_in_dim(query, owner_index * own_heads * HD, own_heads * HD, 1)
     own_query = own_query.reshape(local_rows, own_heads, HD).astype(jnp.float32)
     kv_index = (owner_index * own_heads + jnp.arange(own_heads, dtype=jnp.int32)) // grouping
@@ -127,42 +115,51 @@
         head_out * old_factor[..., None] + own_rounded[..., None] * new_values
     ) / denominator[..., None]
     attended = attended.astype(jnp.bfloat16).reshape(local_rows, own_heads * HD)
+
     proj_terms = jnp.dot(attended, out_weight, preferred_element_type=jnp.float32)
-    projected = lax.psum(proj_terms, "expert")
-    stream = residual.astype(jnp.float32) + projected
+    proj_blocks = proj_terms.reshape(local_rows, owners, columns).transpose(1, 0, 2)
+    projected_cols = jnp.sum(spread_to_owners(proj_blocks, "expert"), axis=0)
+    attn_cols = projected_cols.astype(jnp.bfloat16)
+    residual_cols = lax.dynamic_slice_in_dim(residual, owner_index * columns, columns, 1)
+    stream_cols = residual_cols.astype(jnp.float32) + projected_cols
+    stream = gather_from_all(stream_cols, "expert").transpose(1, 0, 2).reshape(
+        local_rows, model_width
+    )
     inverse = lax.rsqrt(jnp.sum(stream * stream, axis=1, keepdims=True) / model_width + 1e-06)
     normed = (stream * inverse).astype(jnp.bfloat16)
-    attn_cols = lax.dynamic_slice_in_dim(projected, owner_index * columns, columns, 1).astype(
-        jnp.bfloat16
-    )
+
     top_k = route_ids.shape[1]
     experts_total = w_gate.shape[0] * owners
     capacity = max(2, 2 * local_rows * top_k // experts_total)
     own_ids = lax.dynamic_slice_in_dim(route_ids, group_index * local_rows, local_rows, 0)
     own_gates = lax.dynamic_slice_in_dim(route_weights, group_index * local_rows, local_rows, 0)
-    matched = (own_ids == owner_index).astype(jnp.int32).reshape(-1)
-    ranking = jnp.cumsum(matched) - 1
+    expert_ids = jnp.arange(experts_total, dtype=jnp.int32)
+    matched = (own_ids[:, :, None] == expert_ids[None, None, :]).astype(jnp.int32)
+    flat_matched = matched.reshape(local_rows * top_k, experts_total)
+    ranking = jnp.cumsum(flat_matched, axis=0) - 1
     slot_ids = jnp.arange(capacity, dtype=jnp.int32)
-    onehot = ((matched[:, None] == 1) & (ranking[:, None] == slot_ids[None, :])).astype(jnp.float32)
-    chosen = onehot.reshape(local_rows, top_k, capacity)
-    dispatch = jnp.sum(chosen, axis=1).T
-    slot_gate = jnp.sum(chosen * own_gates[:, :, None], axis=(0, 1))
-    dispatch, slot_gate = (dispatch, slot_gate)
+    hit = (flat_matched[:, :, None] == 1) & (ranking[:, :, None] == slot_ids[None, None, :])
+    hit = hit.astype(jnp.float32).reshape(local_rows, top_k, experts_total, capacity)
+    slot_weight = jnp.sum(hit * own_gates[:, :, None, None], axis=1)
+    own_hit = lax.dynamic_index_in_dim(hit, owner_index, 2, False)
+    dispatch = jnp.sum(own_hit, axis=1).T
     routed = jnp.dot(
         dispatch.astype(jnp.bfloat16), normed, preferred_element_type=jnp.float32
     ).astype(jnp.bfloat16)
-    piece = lax.all_gather(routed, "dp", axis=0, tiled=True)
+    piece = gather_from_all(routed, "dp").reshape(groups * capacity, model_width)
     gate_proj = jnp.dot(piece, w_gate[0], preferred_element_type=jnp.float32)
     up_proj = jnp.dot(piece, w_up[0], preferred_element_type=jnp.float32)
     hidden = (jax.nn.silu(gate_proj) * up_proj).astype(jnp.bfloat16)
     outputs = jnp.dot(hidden, w_down[0], preferred_element_type=jnp.float32)
-    summed = lax.psum_scatter(
-        outputs.astype(jnp.bfloat16), "dp", scatter_dimension=0, tiled=True
-    ).astype(jnp.float32)
-    spread = jnp.dot(dispatch.T * slot_gate[None, :], summed, precision=lax.Precision.HIGHEST)
-    mix_cols = lax.psum_scatter(spread, "expert", scatter_dimension=1, tiled=True).astype(
-        jnp.bfloat16
+    partials = spread_to_owners(
+        outputs.astype(jnp.bfloat16).reshape(groups, capacity, model_width), "dp"
     )
+    summed = jnp.sum(partials.astype(jnp.float32), axis=0)
+    slot_blocks = summed.reshape(capacity, owners, columns).transpose(1, 0, 2)
+    got_slots = spread_to_owners(slot_blocks, "expert")
+    mix_cols = jnp.einsum(
+        "tes,esc->tc", slot_weight, got_slots, precision=lax.Precision.HIGHEST
+    ).astype(jnp.bfloat16)
     return (attn_cols, mix_cols)
 
 

time: 690 us -> 175 us (0.25)
  waiting for transfers between devices: 430 us -> 57.9 us
  other arithmetic: 100 us -> 10.1 us
  blocking collectives: 100 us -> 44.7 us
  starting transfers between devices: 11 us -> 42.3 us
  between operations: 14.7 us -> 1.08 us
  matrix products: 11.9 us -> 3.54 us
    unnamed x6 -> x0, waiting for transfers between devices: 220 us -> none
    psum x1 -> x0, waiting for transfers between devices: 183 us -> none  [shards(): projected = lax.psum(proj_terms, 'expert')]
    all_gather x3 -> x0, blocking collectives: 100 us -> none  [the longest x2 79.6 us: combined_all(): lax.all_gather(a.astype(kind), axis)]
    add x126 -> x1, other arithmetic: 92.8 us -> 1.29 us  [shards(): stream_cols = residual_cols.astype(jnp.float32) + projected_cols]
    all_to_all x0 -> x5, waiting for transfers between devices: none -> 52.2 us  [spread_to_owners(): return lax.all_to_all(blocks, axis, 0, 0, tiled=True)]
    all_to_all x0 -> x3, blocking collectives: none -> 44.7 us  [spread_to_owners(): return lax.all_to_all(blocks, axis, 0, 0, tiled=True)]
    all_to_all x0 -> x5, starting transfers between devices: none -> 31.4 us  [spread_to_owners(): return lax.all_to_all(blocks, axis, 0, 0, tiled=True)]
    all_gather x1 -> x0, waiting for transfers between devices: 21.4 us -> none  [combined_all(): lax.all_gather(a.astype(kind), axis)]
  transfers between devices with their start and end apart: 5 -> 6, of which waited for: 5 -> 6; matrix products, arithmetic and copies ran while one was open for 2% -> 6% of each run, Pallas kernels for 0% -> 0%
where the time goes in v1:
time: 175 us; the launch traced here: 174 us
  waiting for transfers between devices  57.9 us (33%)
  blocking collectives  44.7 us (26%)
  starting transfers between devices  42.3 us (24%)
  local copies, waits for them, and re-layouts  14.7 us (8%)
  other arithmetic  10.1 us (6%)
  matrix products  3.54 us (2%)
    all_to_all x5, waiting for transfers between devices, spread_to_owners(): return lax.all_to_all(blocks, axis, 0, 0, tiled=True)  52.2 us
    all_to_all x3, blocking collectives, spread_to_owners(): return lax.all_to_all(blocks, axis, 0, 0, tiled=True)  44.7 us
    all_to_all x5, starting transfers between devices, spread_to_owners(): return lax.all_to_all(blocks, axis, 0, 0, tiled=True)  31.4 us
    all_to_all x1, starting transfers between devices, shards(): lax.all_to_all(send_rows, 'dp', split_axis=0, concat_axis=0, tiled=True)  10.9 us
    unnamed x35, local copies, waits for them, and re-layouts  6.4 us
    all_to_all x1, waiting for transfers between devices, shards(): lax.all_to_all(send_rows, 'dp', split_axis=0, concat_axis=0, tiled=True)  5.7 us
  transfers between devices with their start and end apart: 6, of which 6 were waited for; matrix products, arithmetic and copies ran while one was open for 6% of the time, Pallas kernels for 0%

profile of v1, /device:TPU:1, one launch (start us, length us, event | category | flops | bytes accessed | tf_op | source)
XLA Modules:
  0.0 174.4 jit_solution(3267537696407153973)
XLA Ops:
  0.7 1.1 copy.126
  3.4 10.9 %all-to-all-start = ((bf16[8,16,1024]{2,1,0:T(8,128)(2,1)}), bf16[8,16,1024]{2,1,0:T(8,128)(2,1)S(1)}, u32[]{:S(2)}, u32[]{:S(2)}) async-start(bf16[8,16,1024]{2,1,0:T(8,128)(2,1)} %broadcast_select_fusion), calls=%async_computation | async-start | bytes 524288 | tf_op jit(solution)/shard_map/all_to_all | solution.py:61
  17.2 1.6 copy.82
  18.9 5.7 %all-to-all-done = bf16[8,16,1024]{2,1,0:T(8,128)(2,1)S(1)} async-done(((bf16[8,16,1024]{2,1,0:T(8,128)(2,1)}), bf16[8,16,1024]{2,1,0:T(8,128)(2,1)S(1)}, u32[]{:S(2)}, u32[]{:S(2)}) %all-to-all-start) | async-done | bytes 262176 | tf_op jit(solution)/shard_map/all_to_all | solution.py:61
  26.6 12.6 %all-to-all-start.2 = ((f32[64,16,1]{1,2,0:T(1,128)}), f32[64,16,1]{1,2,0:T(1,128)S(1)}, u32[]{:S(2)}, u32[]{:S(2)}) async-start(f32[64,16,1]{1,2,0:T(1,128)} %bitcast.7), calls=%async_computation.2 | async-start | bytes 65536 | tf_op jit(solution)/shard_map/all_to_all | solution.py:13
  41.4 7.2 %all-to-all-done.2 = f32[64,16,1]{1,2,0:T(1,128)S(1)} async-done(((f32[64,16,1]{1,2,0:T(1,128)}), f32[64,16,1]{1,2,0:T(1,128)S(1)}, u32[]{:S(2)}, u32[]{:S(2)}) %all-to-all-start.2) | async-done | bytes 4128 | tf_op jit(solution)/shard_map/all_to_all | solution.py:13
  48.6 4.7 %all-to-all-start.3 = ((f32[64,16,1]{1,2,0:T(1,128)}), f32[64,16,1]{1,2,0:T(1,128)S(1)}, u32[]{:S(2)}, u32[]{:S(2)}) async-start(f32[64,16,1]{1,2,0:T(1,128)} %bitcast.20), calls=%async_computation.3 | async-start | bytes 65536 | tf_op jit(solution)/shard_map/all_to_all | solution.py:13
  53.4 9.4 %all-to-all-done.3 = f32[64,16,1]{1,2,0:T(1,128)S(1)} async-done(((f32[64,16,1]{1,2,0:T(1,128)}), f32[64,16,1]{1,2,0:T(1,128)S(1)}, u32[]{:S(2)}, u32[]{:S(2)}) %all-to-all-start.3) | async-done | bytes 4128 | tf_op jit(solution)/shard_map/all_to_all | solution.py:13
  62.8 4.7 %all-to-all-start.1 = ((bf16[64,16,1,128]{3,1,2,0:T(8,128)(2,1)}), bf16[64,16,1,128]{3,1,2,0:T(8,128)(2,1)S(1)}, u32[]{:S(2)}, u32[]{:S(2)}) async-start(bf16[64,16,1,128]{3,1,2,0:T(8,128)(2,1)} %bitcast.95), calls=%async_computation.1 | async-start | bytes 524288 | tf_op jit(solution)/shard_map/all_to_all | solution.py:13
  67.6 13.1 %all-to-all-done.1 = bf16[64,16,1,128]{3,1,2,0:T(8,128)(2,1)S(1)} async-done(((bf16[64,16,1,128]{3,1,2,0:T(8,128)(2,1)}), bf16[64,16,1,128]{3,1,2,0:T(8,128)(2,1)S(1)}, u32[]{:S(2)}, u32[]{:S(2)}) %all-to-all-start.1) | async-done | bytes 262176 | tf_op jit(solution)/shard_map/all_to_all | solution.py:13
  81.9 1.0 reshape.429
  83.0 4.7 %all-to-all-start.4 = ((f32[64,1,1024]{2,1,0:T(1,128)}), f32[64,1,1024]{2,1,0:T(1,128)S(1)}, u32[]{:S(2)}, u32[]{:S(2)}) async-start(f32[64,1,1024]{2,1,0:T(1,128)} %reshape.429), calls=%async_computation.4 | async-start | bytes 524288 | tf_op jit(solution)/shard_map/all_to_all | solution.py:13
  88.0 2.7 %add_reduce_fusion = s32[128,64]{1,0:T(8,128)S(1)} fusion(s32[128]{0:T(128)S(1)} %eq.62), kind=kOutput, calls=%fused_computation.7 | output fusion | flops 1064960 | bytes 33280 | tf_op jit(solution)/shard_map/jit(cumsum)/reduce_window_sum | solution.py:139
  90.7 10.2 %all-to-all-done.4 = f32[64,1,1024]{2,1,0:T(1,128)S(1)} async-done(((f32[64,1,1024]{2,1,0:T(1,128)}), f32[64,1,1024]{2,1,0:T(1,128)S(1)}, u32[]{:S(2)}, u32[]{:S(2)}) %all-to-all-start.4) | async-done | bytes 262176 | tf_op jit(solution)/shard_map/all_to_all | solution.py:13
  101.4 1.2 reduce.8
  102.9 1.3 convert_add_fusion
  104.2 1.0 reshape.431
  105.3 4.7 %all-to-all-start.5 = ((f32[64,1,1024]{2,1,0:T(1,128)}), f32[64,1,1024]{2,1,0:T(1,128)S(1)}, u32[]{:S(2)}, u32[]{:S(2)}) async-start(f32[64,1,1024]{2,1,0:T(1,128)} %reshape.431), calls=%async_computation.5 | async-start | bytes 524288 | tf_op jit(solution)/shard_map/all_to_all | solution.py:13
  110.8 12.3 %all-to-all-done.5 = f32[64,1,1024]{2,1,0:T(1,128)S(1)} async-done(((f32[64,1,1024]{2,1,0:T(1,128)}), f32[64,1,1024]{2,1,0:T(1,128)S(1)}, u32[]{:S(2)}, u32[]{:S(2)}) %all-to-all-start.5) | async-done | bytes 262176 | tf_op jit(solution)/shard_map/all_to_all | solution.py:13
  123.1 1.2 reduce.9
  125.4 15.4 %all_to_all.45 = bf16[8,4,4096]{2,1,0:T(4,128)(2,1)} all-to-all(bf16[8,4,4096]{2,1,0:T(4,128)(2,1)S(1)} %broadcast_in_dim.95), channel_id=1, replica_groups=mesh['dp'=8,'expert'=64] {'dp'}, dimensions={0} | all-to-all | bytes 524288 | tf_op jit(solution)/shard_map/all_to_all | solution.py:13
  140.8 1.1 reshape.323
  142.9 14.7 %all_to_all.46 = bf16[8,4,4096]{2,1,0:T(4,128)(2,1)S(1)} all-to-all(bf16[8,4,4096]{2,1,0:T(4,128)(2,1)S(1)} %reshape.324), channel_id=1, replica_groups=mesh['dp'=8,'expert'=64] {'dp'}, dimensions={0} | all-to-all | bytes 524288 | tf_op jit(solution)/shard_map/all_to_all | solution.py:13
  158.0 14.6 %all_to_all.47 = f32[64,1,256]{2,1,0:T(1,128)S(1)} all-to-all(f32[64,1,256]{2,1,0:T(1,128)S(1)} %reshape.433), channel_id=1, replica_groups=mesh['dp'=8,'expert'=64] {'expert'}, dimensions={0} | all-to-all | bytes 131072 | tf_op jit(solution)/shard_map/all_to_all | solution.py:13
  (92 shorter events, 16.0 us)
Async XLA Ops:
  0.6 141.6 %copy-start = (bf16[1,128,4096]{2,1,0:T(8,128)(2,1)S(1)}, bf16[1,128,4096]{2,1,0:T(8,128)(2,1)}, u32[]{:S(2)}) copy-start(bf16[1,128,4096]{2,1,0:T(8,128)(2,1)} %param.29) | copy-start | bytes 3145732
  0.6 1.2 copy-start.10
  0.7 1.8 %copy-start.1 = (s32[64]{0:T(128)S(1)}, s32[64]{0:T(128)}, u32[]{:S(2)}) copy-start(s32[64]{0:T(128)} %param.22) | copy-start | bytes 772
  1.8 12.5 %copy-start.2 = (s32[64]{0:T(128)S(1)}, s32[64]{0:T(128)}, u32[]{:S(2)}) copy-start(s32[64]{0:T(128)} %param.21) | copy-start | bytes 772
  1.9 13.1 %copy-start.7 = (bf16[16,1024]{1,0:T(8,128)(2,1)S(1)}, bf16[16,1024]{1,0:T(8,128)(2,1)}, u32[]{:S(2)}) copy-start(bf16[16,1024]{1,0:T(8,128)(2,1)} %param.17) | copy-start | bytes 98308
  1.9 13.2 %copy-start.5 = (bf16[16,8192]{1,0:T(8,128)(2,1)S(1)}, bf16[16,8192]{1,0:T(8,128)(2,1)}, u32[]{:S(2)}) copy-start(bf16[16,8192]{1,0:T(8,128)(2,1)} %param.16) | copy-start | bytes 786436
  3.4 21.2 %all-to-all-start = ((bf16[8,16,1024]{2,1,0:T(8,128)(2,1)}), bf16[8,16,1024]{2,1,0:T(8,128)(2,1)S(1)}, u32[]{:S(2)}, u32[]{:S(2)}) async-start(bf16[8,16,1024]{2,1,0:T(8,128)(2,1)} %broadcast_select_fusion), calls=%async_computation | async-start | bytes 524288 | tf_op jit(solution)/shard_map/all_to_all | solution.py:61
  17.2 1.6 copy-start.11
  24.7 1.0 copy-start.6
  26.6 22.0 %all-to-all-start.2 = ((f32[64,16,1]{1,2,0:T(1,128)}), f32[64,16,1]{1,2,0:T(1,128)S(1)}, u32[]{:S(2)}, u32[]{:S(2)}) async-start(f32[64,16,1]{1,2,0:T(1,128)} %bitcast.7), calls=%async_computation.2 | async-start | bytes 65536 | tf_op jit(solution)/shard_map/all_to_all | solution.py:13
  48.6 14.2 %all-to-all-start.3 = ((f32[64,16,1]{1,2,0:T(1,128)}), f32[64,16,1]{1,2,0:T(1,128)S(1)}, u32[]{:S(2)}, u32[]{:S(2)}) async-start(f32[64,16,1]{1,2,0:T(1,128)} %bitcast.20), calls=%async_computation.3 | async-start | bytes 65536 | tf_op jit(solution)/shard_map/all_to_all | solution.py:13
  62.8 18.0 %all-to-all-start.1 = ((bf16[64,16,1,128]{3,1,2,0:T(8,128)(2,1)}), bf16[64,16,1,128]{3,1,2,0:T(8,128)(2,1)S(1)}, u32[]{:S(2)}, u32[]{:S(2)}) async-start(bf16[64,16,1,128]{3,1,2,0:T(8,128)(2,1)} %bitcast.95), calls=%async_computation.1 | async-start | bytes 524288 | tf_op jit(solution)/shard_map/all_to_all | solution.py:13
  81.9 5.8 %copy-start.8 = (s32[128,8]{0,1:T(8,128)S(1)}, s32[128,8]{0,1:T(8,128)}, u32[]{:S(2)}) copy-start(s32[128,8]{0,1:T(8,128)} %param.25) | copy-start | bytes 12292
  83.0 17.9 %all-to-all-start.4 = ((f32[64,1,1024]{2,1,0:T(1,128)}), f32[64,1,1024]{2,1,0:T(1,128)S(1)}, u32[]{:S(2)}, u32[]{:S(2)}) async-start(f32[64,1,1024]{2,1,0:T(1,128)} %reshape.429), calls=%async_computation.4 | async-start | bytes 524288 | tf_op jit(solution)/shard_map/all_to_all | solution.py:13
  102.9 7.1 %copy-start.9 = (f32[128,8]{0,1:T(8,128)S(1)}, f32[128,8]{0,1:T(8,128)}, u32[]{:S(2)}) copy-start(f32[128,8]{0,1:T(8,128)} %param.26) | copy-start | bytes 12292
  105.3 17.9 %all-to-all-start.5 = ((f32[64,1,1024]{2,1,0:T(1,128)}), f32[64,1,1024]{2,1,0:T(1,128)S(1)}, u32[]{:S(2)}, u32[]{:S(2)}) async-start(f32[64,1,1024]{2,1,0:T(1,128)} %reshape.431), calls=%async_computation.5 | async-start | bytes 524288 | tf_op jit(solution)/shard_map/all_to_all | solution.py:13
  124.9 17.0 %copy-start.3 = (bf16[1,4096,128]{2,1,0:T(8,128)(2,1)S(1)}, bf16[1,4096,128]{2,1,0:T(8,128)(2,1)}, u32[]{:S(2)}) copy-start(bf16[1,4096,128]{2,1,0:T(8,128)(2,1)} %param.27) | copy-start | bytes 3145732
  140.8 1.4 copy-start.4

commit v2 on v1

--- a/solution.py
+++ b/solution.py
@@ -11,12 +11,6 @@
 
 def spread_to_owners(blocks, axis):
     return lax.all_to_all(blocks, axis, 0, 0, tiled=True)
-
-
-def gather_from_all(block, axis):
-    count = lax.axis_size(axis)
-    stacked = jnp.broadcast_to(block[None], (count,) + block.shape)
-    return spread_to_owners(stacked, axis)
 
 
 def shards(
@@ -85,12 +79,22 @@
         preferred_element_type=jnp.float32,
     )
 
+    head_block = local_rows * own_heads
     send_out = partial_out.reshape(local_rows, owners, own_heads, HD).transpose(1, 0, 2, 3)
     send_peak = highest.reshape(local_rows, owners, own_heads).transpose(1, 0, 2)
     send_sum = weight_sum.reshape(local_rows, owners, own_heads).transpose(1, 0, 2)
-    got_out = spread_to_owners(send_out.astype(jnp.bfloat16), "expert").astype(jnp.float32)
-    got_peak = spread_to_owners(send_peak, "expert")
-    got_sum = spread_to_owners(send_sum, "expert")
+    packed = jnp.concatenate(
+        [
+            send_out.reshape(owners, head_block * HD),
+            send_peak.reshape(owners, head_block),
+            send_sum.reshape(owners, head_block),
+        ],
+        axis=1,
+    )
+    got = spread_to_owners(packed, "expert")
+    got_out = got[:, : head_block * HD].reshape(owners, local_rows, own_heads, HD)
+    got_peak = got[:, head_block * HD : head_block * (HD + 1)].reshape(owners, local_rows, own_heads)
+    got_sum = got[:, head_block * (HD + 1) :].reshape(owners, local_rows, own_heads)
     head_peak = jnp.max(got_peak, axis=0)
     factors = jnp.exp(got_peak - head_peak[None])
     head_out = jnp.sum(got_out * factors[..., None], axis=0)
@@ -122,11 +126,6 @@
     attn_cols = projected_cols.astype(jnp.bfloat16)
     residual_cols = lax.dynamic_slice_in_dim(residual, owner_index * columns, columns, 1)
     stream_cols = residual_cols.astype(jnp.float32) + projected_cols
-    stream = gather_from_all(stream_cols, "expert").transpose(1, 0, 2).reshape(
-        local_rows, model_width
-    )
-    inverse = lax.rsqrt(jnp.sum(stream * stream, axis=1, keepdims=True) / model_width + 1e-06)
-    normed = (stream * inverse).astype(jnp.bfloat16)
 
     top_k = route_ids.shape[1]
     experts_total = w_gate.shape[0] * owners
@@ -139,26 +138,35 @@
     ranking = jnp.cumsum(flat_matched, axis=0) - 1
     slot_ids = jnp.arange(capacity, dtype=jnp.int32)
     hit = (flat_matched[:, :, None] == 1) & (ranking[:, :, None] == slot_ids[None, None, :])
-    hit = hit.astype(jnp.float32).reshape(local_rows, top_k, experts_total, capacity)
-    slot_weight = jnp.sum(hit * own_gates[:, :, None, None], axis=1)
-    own_hit = lax.dynamic_index_in_dim(hit, owner_index, 2, False)
-    dispatch = jnp.sum(own_hit, axis=1).T
-    routed = jnp.dot(
-        dispatch.astype(jnp.bfloat16), normed, preferred_element_type=jnp.float32
-    ).astype(jnp.bfloat16)
-    piece = gather_from_all(routed, "dp").reshape(groups * capacity, model_width)
+    hit = hit.astype(jnp.int32).reshape(local_rows, top_k, experts_total, capacity)
+    slot_weight = jnp.sum(hit.astype(jnp.float32) * own_gates[:, :, None, None], axis=1)
+    slot_token = jnp.sum(hit, axis=1)
+    token_ids = jnp.arange(local_rows, dtype=jnp.int32)
+    slot_source = jnp.sum(slot_token * token_ids[:, None, None], axis=0)
+    slot_used = jnp.sum(slot_token, axis=0) > 0
+
+    slot_cols = jnp.where(slot_used[:, :, None], stream_cols[slot_source], 0.0)
+    slot_cols = jnp.broadcast_to(slot_cols[None], (groups,) + slot_cols.shape)
+    slot_cols = slot_cols.reshape(groups * experts_total, capacity, columns)
+    rows_in = spread_to_owners(slot_cols, ("dp", "expert"))
+    rows_in = rows_in.reshape(groups, owners, capacity, columns).transpose(0, 2, 1, 3)
+    stream_rows = rows_in.reshape(groups * capacity, model_width)
+    inverse = lax.rsqrt(
+        jnp.sum(stream_rows * stream_rows, axis=1, keepdims=True) / model_width + 1e-06
+    )
+    piece = (stream_rows * inverse).astype(jnp.bfloat16)
     gate_proj = jnp.dot(piece, w_gate[0], preferred_element_type=jnp.float32)
     up_proj = jnp.dot(piece, w_up[0], preferred_element_type=jnp.float32)
     hidden = (jax.nn.silu(gate_proj) * up_proj).astype(jnp.bfloat16)
     outputs = jnp.dot(hidden, w_down[0], preferred_element_type=jnp.float32)
-    partials = spread_to_owners(
-        outputs.astype(jnp.bfloat16).reshape(groups, capacity, model_width), "dp"
-    )
+
+    out_blocks = outputs.astype(jnp.bfloat16).reshape(groups, capacity, owners, columns)
+    out_blocks = out_blocks.transpose(0, 2, 1, 3).reshape(groups * owners, capacity, columns)
+    partials = spread_to_owners(out_blocks, ("dp", "expert"))
+    partials = partials.reshape(groups, experts_total, capacity, columns)
     summed = jnp.sum(partials.astype(jnp.float32), axis=0)
-    slot_blocks = summed.reshape(capacity, owners, columns).transpose(1, 0, 2)
-    got_slots = spread_to_owners(slot_blocks, "expert")
     mix_cols = jnp.einsum(
-        "tes,esc->tc", slot_weight, got_slots, precision=lax.Precision.HIGHEST
+        "tes,esc->tc", slot_weight, summed, precision=lax.Precision.HIGHEST
     ).astype(jnp.bfloat16)
     return (attn_cols, mix_cols)
 

time: 175 us -> 154 us (0.88)
  blocking collectives: 44.7 us -> 31.7 us
  waiting for transfers between devices: 57.9 us -> 51.7 us
  starting transfers between devices: 42.3 us -> 38 us
  local copies, waits for them, and re-layouts: 14.7 us -> 16.6 us
    all_to_all x3 -> x1, blocking collectives: 44.7 us -> 31.7 us  [spread_to_owners(): return lax.all_to_all(blocks, axis, 0, 0, tiled=True)]
    all_to_all x5 -> x3, waiting for transfers between devices: 52.2 us -> 43.4 us  [spread_to_owners(): return lax.all_to_all(blocks, axis, 0, 0, tiled=True)]
    all_to_all x5 -> x3, starting transfers between devices: 31.4 us -> 27.1 us  [spread_to_owners(): return lax.all_to_all(blocks, axis, 0, 0, tiled=True)]
    all_to_all x1, waiting for transfers between devices: 5.7 us -> 8.25 us  [shards(): lax.all_to_all(send_rows, 'dp', split_axis=0, concat_axis=0, tiled=True)]
    unnamed x35 -> x32, local copies, waits for them, and re-layouts: 6.4 us -> 6.89 us
  transfers between devices with their start and end apart: 6 -> 4, of which waited for: 6 -> 4; matrix products, arithmetic and copies ran while one was open for 6% -> 5% of each run, Pallas kernels for 0% -> 0%
where the time goes in v2:
time: 154 us
  waiting for transfers between devices  51.7 us (34%)
  starting transfers between devices  38 us (25%)
  blocking collectives  31.7 us (21%)
  local copies, waits for them, and re-layouts  16.6 us (11%)
  other arithmetic  10.3 us (7%)
  matrix products  4.46 us (3%)
    all_to_all x3, waiting for transfers between devices, spread_to_owners(): return lax.all_to_all(blocks, axis, 0, 0, tiled=True)  43.4 us
    all_to_all x1, blocking collectives, spread_to_owners(): return lax.all_to_all(blocks, axis, 0, 0, tiled=True)  31.7 us
    all_to_all x3, starting transfers between devices, spread_to_owners(): return lax.all_to_all(blocks, axis, 0, 0, tiled=True)  27.1 us
    all_to_all x1, starting transfers between devices, shards(): lax.all_to_all(send_rows, 'dp', split_axis=0, concat_axis=0, tiled=True)  10.9 us
    all_to_all x1, waiting for transfers between devices, shards(): lax.all_to_all(send_rows, 'dp', split_axis=0, concat_axis=0, tiled=True)  8.25 us
    unnamed x32, local copies, waits for them, and re-layouts  6.89 us
    all_to_all x2, other arithmetic, spread_to_owners(): return lax.all_to_all(blocks, axis, 0, 0, tiled=True)  3.14 us
  transfers between devices with their start and end apart: 4, of which 4 were waited for; matrix products, arithmetic and copies ran while one was open for 5% of the time, Pallas kernels for 0%

profile of v2, /device:TPU:1, one launch (start us, length us, event | category | flops | bytes accessed | tf_op | source)
XLA Modules:
  0.0 153.7 jit_solution(5196315242562585822)
XLA Ops:
  0.7 1.1 copy.138
  2.6 0.8 broadcast_select_fusion
  3.3 10.9 %all-to-all-start = ((bf16[8,16,1024]{2,1,0:T(8,128)(2,1)}), bf16[8,16,1024]{2,1,0:T(8,128)(2,1)S(1)}, u32[]{:S(2)}, u32[]{:S(2)}) async-start(bf16[8,16,1024]{2,1,0:T(8,128)(2,1)} %broadcast_select_fusion), calls=%async_computation | async-start | bytes 524288 | tf_op jit(solution)/shard_map/all_to_all | solution.py:55
  16.3 8.3 %all-to-all-done = bf16[8,16,1024]{2,1,0:T(8,128)(2,1)S(1)} async-done(((bf16[8,16,1024]{2,1,0:T(8,128)(2,1)}), bf16[8,16,1024]{2,1,0:T(8,128)(2,1)S(1)}, u32[]{:S(2)}, u32[]{:S(2)}) %all-to-all-start) | async-done | bytes 262176 | tf_op jit(solution)/shard_map/all_to_all | solution.py:55
  24.7 0.8 scatter_fusion
  27.1 1.4 copy.75
  28.5 12.6 %all-to-all-start.1 = ((f32[64,1,2080]{2,1,0:T(1,128)}), f32[64,1,2080]{2,1,0:T(1,128)S(1)}, u32[]{:S(2)}, u32[]{:S(2)}) async-start(f32[64,1,2080]{2,1,0:T(1,128)} %copy.75), calls=%async_computation.1 | async-start | bytes 1114112 | tf_op jit(solution)/shard_map/all_to_all | solution.py:13
  41.3 1.6 %copy.78 = bf16[128,4096]{0,1:T(8,128)(2,1)S(1)} copy(bf16[128,4096]{1,0:T(8,128)(2,1)} %param.23) | data formatting | bytes 2097152 | tf_op args[7]
  43.2 2.7 %add_reduce_fusion = s32[128,64]{1,0:T(8,128)S(1)} fusion(s32[128]{0:T(128)S(1)} %eq.62), kind=kOutput, calls=%fused_computation.7 | output fusion | flops 1064960 | bytes 33280 | tf_op jit(solution)/shard_map/jit(cumsum)/reduce_window_sum | solution.py:138
  46.1 13.4 %all-to-all-done.1 = f32[64,1,2080]{2,1,0:T(1,128)S(1)} async-done(((f32[64,1,2080]{2,1,0:T(1,128)}), f32[64,1,2080]{2,1,0:T(1,128)S(1)}, u32[]{:S(2)}, u32[]{:S(2)}) %all-to-all-start.1) | async-done | bytes 532512 | tf_op jit(solution)/shard_map/all_to_all | solution.py:13
  60.0 0.9 convolution_bitcast_fusion
  61.0 1.0 reshape.505
  62.0 5.7 %all-to-all-start.2 = ((f32[64,1,1024]{2,1,0:T(1,128)}), f32[64,1,1024]{2,1,0:T(1,128)S(1)}, u32[]{:S(2)}, u32[]{:S(2)}) async-start(f32[64,1,1024]{2,1,0:T(1,128)} %reshape.505), calls=%async_computation.2 | async-start | bytes 524288 | tf_op jit(solution)/shard_map/all_to_all | solution.py:13
  68.2 12.8 %all-to-all-done.2 = f32[64,1,1024]{2,1,0:T(1,128)S(1)} async-done(((f32[64,1,1024]{2,1,0:T(1,128)}), f32[64,1,1024]{2,1,0:T(1,128)S(1)}, u32[]{:S(2)}, u32[]{:S(2)}) %all-to-all-start.2) | async-done | bytes 262176 | tf_op jit(solution)/shard_map/all_to_all | solution.py:13
  81.4 1.3 reduce.11
  82.9 1.3 convert_add_fusion
  85.2 1.0 reshape.507
  86.2 31.7 %all_to_all.32 = f32[512,1,256]{2,1,0:T(1,128)S(1)} all-to-all(f32[512,1,256]{2,1,0:T(1,128)S(1)} %reshape.507), channel_id=1, replica_groups=mesh['dp'=8,'expert'=64] {'dp','expert'}, dimensions={0} | all-to-all | bytes 1048576 | tf_op jit(solution)/shard_map/all_to_all | solution.py:13
  117.9 1.9 %reduce.12 = f32[512,256]{1,0:T(8,128)S(1)} reduce(f32[512,1,256]{2,1,0:T(1,128)S(1)} %all_to_all.32, f32[]{:T(128)} %broadcast.362), dimensions={1}, to_apply=%all_to_all.25.reduce_sub_computation | reduce | bytes 1048580 | tf_op jit(solution)/shard_map/all_to_all | solution.py:13
  122.0 1.5 fusion.10
  125.0 0.9 reshape.509
  126.0 8.8 %all-to-all-start.4 = ((bf16[512,2,128]{2,1,0:T(2,128)(2,1)}), bf16[512,2,128]{2,1,0:T(2,128)(2,1)S(1)}, u32[]{:S(2)}, u32[]{:S(2)}) async-start(bf16[512,2,128]{2,1,0:T(2,128)(2,1)} %reshape.509), calls=%async_computation.4 | async-start | bytes 524288 | tf_op jit(solution)/shard_map/all_to_all | solution.py:13
  135.1 17.3 %all-to-all-done.4 = bf16[512,2,128]{2,1,0:T(2,128)(2,1)S(1)} async-done(((bf16[512,2,128]{2,1,0:T(2,128)(2,1)}), bf16[512,2,128]{2,1,0:T(2,128)(2,1)S(1)}, u32[]{:S(2)}, u32[]{:S(2)}) %all-to-all-start.4) | async-done | bytes 262176 | tf_op jit(solution)/shard_map/all_to_all | solution.py:13
  152.9 0.8 fusion.6
  (91 shorter events, 12.3 us)
Async XLA Ops:
  0.6 122.8 %copy-start = (bf16[1,128,4096]{2,1,0:T(8,128)(2,1)S(1)}, bf16[1,128,4096]{2,1,0:T(8,128)(2,1)}, u32[]{:S(2)}) copy-start(bf16[1,128,4096]{2,1,0:T(8,128)(2,1)} %param.29) | copy-start | bytes 3145732
  0.6 1.1 copy-start.8
  0.7 1.2 copy-start.1
  2.0 12.9 %copy-start.2 = (s32[64]{0:T(128)S(1)}, s32[64]{0:T(128)}, u32[]{:S(2)}) copy-start(s32[64]{0:T(128)} %param.21) | copy-start | bytes 772
  2.5 13.1 %copy-start.4 = (bf16[16,8192]{1,0:T(8,128)(2,1)S(1)}, bf16[16,8192]{1,0:T(8,128)(2,1)}, u32[]{:S(2)}) copy-start(bf16[16,8192]{1,0:T(8,128)(2,1)} %param.16) | copy-start | bytes 786436
  3.3 21.2 %all-to-all-start = ((bf16[8,16,1024]{2,1,0:T(8,128)(2,1)}), bf16[8,16,1024]{2,1,0:T(8,128)(2,1)S(1)}, u32[]{:S(2)}, u32[]{:S(2)}) async-start(bf16[8,16,1024]{2,1,0:T(8,128)(2,1)} %broadcast_select_fusion), calls=%async_computation | async-start | bytes 524288 | tf_op jit(solution)/shard_map/all_to_all | solution.py:55
  14.2 2.0 %copy-start.9 = (s32[16]{0:T(128)S(1)}, s32[16]{0:T(128)}, u32[]{:S(2)}) copy-start(s32[16]{0:T(128)} %param.19) | copy-start | bytes 196
  14.2 2.1 %copy-start.5 = (bf16[16,1024]{1,0:T(8,128)(2,1)S(1)}, bf16[16,1024]{1,0:T(8,128)(2,1)}, u32[]{:S(2)}) copy-start(bf16[16,1024]{1,0:T(8,128)(2,1)} %param.17) | copy-start | bytes 98308
  27.1 14.0 %copy-start.6 = (s32[128,8]{0,1:T(8,128)S(1)}, s32[128,8]{0,1:T(8,128)}, u32[]{:S(2)}) copy-start(s32[128,8]{0,1:T(8,128)} %param.25) | copy-start | bytes 12292
  28.5 31.0 %all-to-all-start.1 = ((f32[64,1,2080]{2,1,0:T(1,128)}), f32[64,1,2080]{2,1,0:T(1,128)S(1)}, u32[]{:S(2)}, u32[]{:S(2)}) async-start(f32[64,1,2080]{2,1,0:T(1,128)} %copy.75), calls=%async_computation.1 | async-start | bytes 1114112 | tf_op jit(solution)/shard_map/all_to_all | solution.py:13
  62.0 18.9 %all-to-all-start.2 = ((f32[64,1,1024]{2,1,0:T(1,128)}), f32[64,1,1024]{2,1,0:T(1,128)S(1)}, u32[]{:S(2)}, u32[]{:S(2)}) async-start(f32[64,1,1024]{2,1,0:T(1,128)} %reshape.505), calls=%async_computation.2 | async-start | bytes 524288 | tf_op jit(solution)/shard_map/all_to_all | solution.py:13
  121.5 2.0 %copy-start.3 = (bf16[1,4096,128]{2,1,0:T(8,128)(2,1)S(1)}, bf16[1,4096,128]{2,1,0:T(8,128)(2,1)}, u32[]{:S(2)}) copy-start(bf16[1,4096,128]{2,1,0:T(8,128)(2,1)} %param.28) | copy-start | bytes 3145732
  124.6 10.1 %copy-start.7 = (f32[128,8]{0,1:T(8,128)S(1)}, f32[128,8]{0,1:T(8,128)}, u32[]{:S(2)}) copy-start(f32[128,8]{0,1:T(8,128)} %param.26) | copy-start | bytes 12292
  126.0 26.4 %all-to-all-start.4 = ((bf16[512,2,128]{2,1,0:T(2,128)(2,1)}), bf16[512,2,128]{2,1,0:T(2,128)(2,1)S(1)}, u32[]{:S(2)}, u32[]{:S(2)}) async-start(bf16[512,2,128]{2,1,0:T(2,128)(2,1)} %reshape.509), calls=%async_computation.4 | async-start | bytes 524288 | tf_op jit(solution)/shard_map/all_to_all | solution.py:13

commit v3 on v2

--- a/solution.py
+++ b/solution.py
@@ -11,6 +11,14 @@
 
 def spread_to_owners(blocks, axis):
     return lax.all_to_all(blocks, axis, 0, 0, tiled=True)
+
+
+def split_three(values):
+    high = lax.reduce_precision(values, exponent_bits=8, mantissa_bits=7)
+    rest = values - high
+    middle = lax.reduce_precision(rest, exponent_bits=8, mantissa_bits=7)
+    low = rest - middle
+    return jnp.stack([high, middle, low]).astype(jnp.bfloat16)
 
 
 def shards(
@@ -83,18 +91,25 @@
     send_out = partial_out.reshape(local_rows, owners, own_heads, HD).transpose(1, 0, 2, 3)
     send_peak = highest.reshape(local_rows, owners, own_heads).transpose(1, 0, 2)
     send_sum = weight_sum.reshape(local_rows, owners, own_heads).transpose(1, 0, 2)
+    stats = jnp.stack([send_peak, send_sum], axis=1).reshape(owners, 2 * head_block)
+    stat_parts = split_three(stats).transpose(1, 0, 2).reshape(owners, 6 * head_block)
+    stat_width = -(-6 * head_block // HD) * HD
+    stat_parts = jnp.pad(stat_parts, ((0, 0), (0, stat_width - 6 * head_block)))
     packed = jnp.concatenate(
         [
-            send_out.reshape(owners, head_block * HD),
-            send_peak.reshape(owners, head_block),
-            send_sum.reshape(owners, head_block),
+            send_out.astype(jnp.bfloat16).reshape(owners, head_block, HD),
+            stat_parts.reshape(owners, stat_width // HD, HD),
         ],
         axis=1,
     )
     got = spread_to_owners(packed, "expert")
-    got_out = got[:, : head_block * HD].reshape(owners, local_rows, own_heads, HD)
-    got_peak = got[:, head_block * HD : head_block * (HD + 1)].reshape(owners, local_rows, own_heads)
-    got_sum = got[:, head_block * (HD + 1) :].reshape(owners, local_rows, own_heads)
+    got_out = got[:, :head_block].astype(jnp.float32).reshape(owners, local_rows, own_heads, HD)
+    got_stats = got[:, head_block:].reshape(owners, stat_width)[:, : 6 * head_block]
+    got_stats = got_stats.reshape(owners, 3, 2 * head_block).astype(jnp.float32)
+    got_stats = (got_stats[:, 0] + got_stats[:, 1]) + got_stats[:, 2]
+    got_stats = got_stats.reshape(owners, 2, local_rows, own_heads)
+    got_peak = got_stats[:, 0]
+    got_sum = got_stats[:, 1]
     head_peak = jnp.max(got_peak, axis=0)
     factors = jnp.exp(got_peak - head_peak[None])
     head_out = jnp.sum(got_out * factors[..., None], axis=0)
@@ -120,9 +135,14 @@
     ) / denominator[..., None]
     attended = attended.astype(jnp.bfloat16).reshape(local_rows, own_heads * HD)
 
-    proj_terms = jnp.dot(attended, out_weight, preferred_element_type=jnp.float32)
-    proj_blocks = proj_terms.reshape(local_rows, owners, columns).transpose(1, 0, 2)
-    projected_cols = jnp.sum(spread_to_owners(proj_blocks, "expert"), axis=0)
+    proj_blocks = jnp.einsum(
+        "bd,doc->obc",
+        attended,
+        out_weight.reshape(own_heads * HD, owners, columns),
+        preferred_element_type=jnp.float32,
+    )
+    got_proj = spread_to_owners(proj_blocks.astype(jnp.bfloat16), "expert")
+    projected_cols = jnp.sum(got_proj.astype(jnp.float32), axis=0)
     attn_cols = projected_cols.astype(jnp.bfloat16)
     residual_cols = lax.dynamic_slice_in_dim(residual, owner_index * columns, columns, 1)
     stream_cols = residual_cols.astype(jnp.float32) + projected_cols
@@ -145,12 +165,12 @@
     slot_source = jnp.sum(slot_token * token_ids[:, None, None], axis=0)
     slot_used = jnp.sum(slot_token, axis=0) > 0
 
-    slot_cols = jnp.where(slot_used[:, :, None], stream_cols[slot_source], 0.0)
+    slot_cols = jnp.where(slot_used[:, :, None], stream_cols[slot_source], 0.0).astype(jnp.bfloat16)
     slot_cols = jnp.broadcast_to(slot_cols[None], (groups,) + slot_cols.shape)
     slot_cols = slot_cols.reshape(groups * experts_total, capacity, columns)
     rows_in = spread_to_owners(slot_cols, ("dp", "expert"))
     rows_in = rows_in.reshape(groups, owners, capacity, columns).transpose(0, 2, 1, 3)
-    stream_rows = rows_in.reshape(groups * capacity, model_width)
+    stream_rows = rows_in.reshape(groups * capacity, model_width).astype(jnp.float32)
     inverse = lax.rsqrt(
         jnp.sum(stream_rows * stream_rows, axis=1, keepdims=True) / model_width + 1e-06
     )

time: 154 us -> 138 us (0.90)
  waiting for transfers between devices: 51.7 us -> 41.4 us
  blocking collectives: 31.7 us -> 26.5 us
    all_to_all x3, waiting for transfers between devices: 43.4 us -> 36.9 us  [spread_to_owners(): return lax.all_to_all(blocks, axis, 0, 0, tiled=True)]
    all_to_all x1, blocking collectives: 31.7 us -> 26.5 us  [spread_to_owners(): return lax.all_to_all(blocks, axis, 0, 0, tiled=True)]
    all_to_all x1, waiting for transfers between devices: 8.25 us -> 4.48 us  [shards(): lax.all_to_all(send_rows, 'dp', split_axis=0, concat_axis=0, tiled=True)]
    all_to_all x2 -> x0, other arithmetic: 3.14 us -> none  [spread_to_owners(): return lax.all_to_all(blocks, axis, 0, 0, tiled=True)]
    unnamed x32 -> x39, local copies, waits for them, and re-layouts: 6.89 us -> 4.8 us
    all_to_all x2 -> x1, local copies, waits for them, and re-layouts: 1.88 us -> 0.3 us  [spread_to_owners(): return lax.all_to_all(blocks, axis, 0, 0, tiled=True)]
  transfers between devices with their start and end apart: 4 -> 4, of which waited for: 4 -> 4; matrix products, arithmetic and copies ran while one was open for 5% -> 9% of each run, Pallas kernels for 0% -> 0%
where the time goes in v3:
time: 138 us; the launch traced here: 137 us
  waiting for transfers between devices  41.4 us (30%)
  starting transfers between devices  37.5 us (27%)
  blocking collectives  26.5 us (19%)
  local copies, waits for them, and re-layouts  15.8 us (11%)
  other arithmetic  10.3 us (7%)
  matrix products  4.55 us (3%)
    all_to_all x3, waiting for transfers between devices, spread_to_owners(): return lax.all_to_all(blocks, axis, 0, 0, tiled=True)  36.9 us
    all_to_all x3, starting transfers between devices, spread_to_owners(): return lax.all_to_all(blocks, axis, 0, 0, tiled=True)  26.6 us
    all_to_all x1, blocking collectives, spread_to_owners(): return lax.all_to_all(blocks, axis, 0, 0, tiled=True)  26.5 us
    all_to_all x1, starting transfers between devices, shards(): lax.all_to_all(send_rows, 'dp', split_axis=0, concat_axis=0, tiled=True)  11 us
    unnamed x39, local copies, waits for them, and re-layouts  4.8 us
    all_to_all x1, waiting for transfers between devices, shards(): lax.all_to_all(send_rows, 'dp', split_axis=0, concat_axis=0, tiled=True)  4.48 us
  transfers between devices with their start and end apart: 4, of which 4 were waited for; matrix products, arithmetic and copies ran while one was open for 9% of the time, Pallas kernels for 0%

profile of v3, /device:TPU:1, one launch (start us, length us, event | category | flops | bytes accessed | tf_op | source)
XLA Modules:
  0.0 137.4 jit_solution(2717695658727157834)
XLA Ops:
  0.7 1.1 copy.155
  2.5 0.8 broadcast_select_fusion
  3.3 11.0 %all-to-all-start = ((bf16[8,16,1024]{2,1,0:T(8,128)(2,1)}), bf16[8,16,1024]{2,1,0:T(8,128)(2,1)S(1)}, u32[]{:S(2)}, u32[]{:S(2)}) async-start(bf16[8,16,1024]{2,1,0:T(8,128)(2,1)} %broadcast_select_fusion), calls=%async_computation | async-start | bytes 524288 | tf_op jit(solution)/shard_map/all_to_all | solution.py:63
  16.0 2.7 %add_reduce_fusion = s32[128,64]{1,0:T(8,128)S(1)} fusion(s32[128]{0:T(128)S(1)} %eq.62), kind=kOutput, calls=%fused_computation.7 | output fusion | flops 1064960 | bytes 33280 | tf_op jit(solution)/shard_map/jit(cumsum)/reduce_window_sum | solution.py:158
  20.2 4.5 %all-to-all-done = bf16[8,16,1024]{2,1,0:T(8,128)(2,1)S(1)} async-done(((bf16[8,16,1024]{2,1,0:T(8,128)(2,1)}), bf16[8,16,1024]{2,1,0:T(8,128)(2,1)S(1)}, u32[]{:S(2)}, u32[]{:S(2)}) %all-to-all-start) | async-done | bytes 262176 | tf_op jit(solution)/shard_map/all_to_all | solution.py:63
  24.8 0.8 scatter_fusion
  27.1 0.8 pad_maximum_fusion
  27.9 12.6 %all-to-all-start.1 = ((bf16[64,17,128]{2,1,0:T(8,128)(2,1)}), bf16[64,17,128]{2,1,0:T(8,128)(2,1)S(1)}, u32[]{:S(2)}, u32[]{:S(2)}) async-start(bf16[64,17,128]{2,1,0:T(8,128)(2,1)} %pad_maximum_fusion), calls=%async_computation.1 | async-start | bytes 786432 | tf_op jit(solution)/shard_map/all_to_all | solution.py:13
  43.1 0.7 constant_dynamic-slice_fusion.1
  44.6 0.8 fusion.37
  45.4 0.8 multiply_reduce_fusion.2
  46.2 9.4 %all-to-all-done.1 = bf16[64,17,128]{2,1,0:T(8,128)(2,1)S(1)} async-done(((bf16[64,17,128]{2,1,0:T(8,128)(2,1)}), bf16[64,17,128]{2,1,0:T(8,128)(2,1)S(1)}, u32[]{:S(2)}, u32[]{:S(2)}) %all-to-all-start.1) | async-done | bytes 278560 | tf_op jit(solution)/shard_map/all_to_all | solution.py:13
  56.4 0.9 fusion.5
  57.4 0.9 reshape.631
  58.2 5.6 %all-to-all-start.2 = ((bf16[64,2,512]{2,1,0:T(2,128)(2,1)}), bf16[64,2,512]{2,1,0:T(2,128)(2,1)S(1)}, u32[]{:S(2)}, u32[]{:S(2)}) async-start(bf16[64,2,512]{2,1,0:T(2,128)(2,1)} %reshape.631), calls=%async_computation.2 | async-start | bytes 262144 | tf_op jit(solution)/shard_map/all_to_all | solution.py:13
  64.0 10.9 %all-to-all-done.2 = bf16[64,2,512]{2,1,0:T(2,128)(2,1)S(1)} async-done(((bf16[64,2,512]{2,1,0:T(2,128)(2,1)}), bf16[64,2,512]{2,1,0:T(2,128)(2,1)S(1)}, u32[]{:S(2)}, u32[]{:S(2)}) %all-to-all-start.2) | async-done | bytes 131104 | tf_op jit(solution)/shard_map/all_to_all | solution.py:13
  75.2 0.8 convert_add_fusion
  76.0 0.9 gather_fusion.4
  77.4 26.5 %all_to_all.25 = bf16[512,2,128]{2,1,0:T(2,128)(2,1)S(1)} all-to-all(bf16[512,2,128]{2,1,0:T(2,128)(2,1)S(1)} %reshape.633), channel_id=1, replica_groups=mesh['dp'=8,'expert'=64] {'dp','expert'}, dimensions={0} | all-to-all | bytes 524288 | tf_op jit(solution)/shard_map/all_to_all | solution.py:13
  106.0 1.5 %fusion.11 = f32[32,128]{1,0:T(8,128)S(1)} fusion(bf16[32,4096]{1,0:T(8,128)(2,1)S(1)} %convert_element_type.158, bf16[1,4096,128]{2,1,0:T(8,128)(2,1)} %param.27), kind=kOutput, calls=%fused_computation.25 | convolution fusion | flops 33554432 | bytes 1327104 | tf_op jit(solution)/shard_map/dot_general | solution.py:178
  109.1 0.9 reshape.635
  110.0 8.4 %all-to-all-start.4 = ((bf16[512,2,128]{2,1,0:T(2,128)(2,1)}), bf16[512,2,128]{2,1,0:T(2,128)(2,1)S(1)}, u32[]{:S(2)}, u32[]{:S(2)}) async-start(bf16[512,2,128]{2,1,0:T(2,128)(2,1)} %reshape.635), calls=%async_computation.4 | async-start | bytes 524288 | tf_op jit(solution)/shard_map/all_to_all | solution.py:13
  119.4 16.7 %all-to-all-done.4 = bf16[512,2,128]{2,1,0:T(2,128)(2,1)S(1)} async-done(((bf16[512,2,128]{2,1,0:T(2,128)(2,1)}), bf16[512,2,128]{2,1,0:T(2,128)(2,1)S(1)}, u32[]{:S(2)}, u32[]{:S(2)}) %all-to-all-start.4) | async-done | bytes 262176 | tf_op jit(solution)/shard_map/all_to_all | solution.py:13
  136.6 0.8 fusion.7
  (107 shorter events, 15.6 us)
Async XLA Ops:
  0.6 106.9 %copy-start = (bf16[1,128,4096]{2,1,0:T(8,128)(2,1)S(1)}, bf16[1,128,4096]{2,1,0:T(8,128)(2,1)}, u32[]{:S(2)}) copy-start(bf16[1,128,4096]{2,1,0:T(8,128)(2,1)} %param.29) | copy-start | bytes 3145732
  0.6 1.2 copy-start.12
  0.7 1.2 copy-start.1
  1.8 12.5 %copy-start.10 = (s32[128,8]{0,1:T(8,128)S(1)}, s32[128,8]{0,1:T(8,128)}, u32[]{:S(2)}) copy-start(s32[128,8]{0,1:T(8,128)} %param.25) | copy-start | bytes 12292
  2.0 13.4 %copy-start.2 = (s32[64]{0:T(128)S(1)}, s32[64]{0:T(128)}, u32[]{:S(2)}) copy-start(s32[64]{0:T(128)} %param.21) | copy-start | bytes 772
  3.3 16.2 %copy-start.7 = (bf16[16,8192]{1,0:T(8,128)(2,1)S(1)}, bf16[16,8192]{1,0:T(8,128)(2,1)}, u32[]{:S(2)}) copy-start(bf16[16,8192]{1,0:T(8,128)(2,1)} %param.16) | copy-start | bytes 786436
  3.3 21.4 %all-to-all-start = ((bf16[8,16,1024]{2,1,0:T(8,128)(2,1)}), bf16[8,16,1024]{2,1,0:T(8,128)(2,1)S(1)}, u32[]{:S(2)}, u32[]{:S(2)}) async-start(bf16[8,16,1024]{2,1,0:T(8,128)(2,1)} %broadcast_select_fusion), calls=%async_computation | async-start | bytes 524288 | tf_op jit(solution)/shard_map/all_to_all | solution.py:63
  14.7 5.4 %copy-start.13 = (s32[16]{0:T(128)S(1)}, s32[16]{0:T(128)}, u32[]{:S(2)}) copy-start(s32[16]{0:T(128)} %param.19) | copy-start | bytes 196
  14.7 5.5 %copy-start.9 = (bf16[16,1024]{1,0:T(8,128)(2,1)S(1)}, bf16[16,1024]{1,0:T(8,128)(2,1)}, u32[]{:S(2)}) copy-start(bf16[16,1024]{1,0:T(8,128)(2,1)} %param.17) | copy-start | bytes 98308
  18.7 0.7 copy-start.5
  26.9 15.5 %copy-start.3 = (bf16[128,4096]{1,0:T(8,128)(2,1)S(1)}, bf16[128,4096]{1,0:T(8,128)(2,1)}, u32[]{:S(2)}) copy-start(bf16[128,4096]{1,0:T(8,128)(2,1)} %param.23) | copy-start | bytes 3145732
  27.9 27.6 %all-to-all-start.1 = ((bf16[64,17,128]{2,1,0:T(8,128)(2,1)}), bf16[64,17,128]{2,1,0:T(8,128)(2,1)S(1)}, u32[]{:S(2)}, u32[]{:S(2)}) async-start(bf16[64,17,128]{2,1,0:T(8,128)(2,1)} %pad_maximum_fusion), calls=%async_computation.1 | async-start | bytes 786432 | tf_op jit(solution)/shard_map/all_to_all | solution.py:13
  57.4 19.5 %copy-start.8 = (pred[64,4]{1,0:T(8,128)(4,1)S(1)}, pred[64,4]{1,0:T(8,128)(4,1)}, u32[]{:S(2)}) copy-start(pred[64,4]{1,0:T(8,128)(4,1)} %copy.106) | copy-start | bytes 772
  58.2 16.7 %all-to-all-start.2 = ((bf16[64,2,512]{2,1,0:T(2,128)(2,1)}), bf16[64,2,512]{2,1,0:T(2,128)(2,1)S(1)}, u32[]{:S(2)}, u32[]{:S(2)}) async-start(bf16[64,2,512]{2,1,0:T(2,128)(2,1)} %reshape.631), calls=%async_computation.2 | async-start | bytes 262144 | tf_op jit(solution)/shard_map/all_to_all | solution.py:13
  105.5 2.0 %copy-start.4 = (bf16[1,4096,128]{2,1,0:T(8,128)(2,1)S(1)}, bf16[1,4096,128]{2,1,0:T(8,128)(2,1)}, u32[]{:S(2)}) copy-start(bf16[1,4096,128]{2,1,0:T(8,128)(2,1)} %param.28) | copy-start | bytes 3145732
  108.6 9.8 %copy-start.11 = (f32[128,8]{0,1:T(8,128)S(1)}, f32[128,8]{0,1:T(8,128)}, u32[]{:S(2)}) copy-start(f32[128,8]{0,1:T(8,128)} %param.26) | copy-start | bytes 12292
  108.7 9.9 %copy-start.6 = (s32[128,64]{1,0:T(8,128)S(1)}, s32[128,64]{1,0:T(8,128)}, u32[]{:S(2)}) copy-start(s32[128,64]{1,0:T(8,128)} %copy-done.5) | copy-start | bytes 98308
  110.0 26.0 %all-to-all-start.4 = ((bf16[512,2,128]{2,1,0:T(2,128)(2,1)}), bf16[512,2,128]{2,1,0:T(2,128)(2,1)S(1)}, u32[]{:S(2)}, u32[]{:S(2)}) async-start(bf16[512,2,128]{2,1,0:T(2,128)(2,1)} %reshape.635), calls=%async_computation.4 | async-start | bytes 524288 | tf_op jit(solution)/shard_map/all_to_all | solution.py:13

commit v4 on v3

--- a/solution.py
+++ b/solution.py
@@ -60,7 +60,9 @@
         kv_cache[outgoing],
         jnp.zeros((), kv_cache.dtype),
     )
-    arrived = lax.all_to_all(send_rows, "dp", split_axis=0, concat_axis=0, tiled=True)
+    fork_shape = send_rows.shape
+    send_rows = send_rows.reshape(fork_shape[0], fork_shape[1] // 2, 2 * fork_shape[2])
+    arrived = spread_to_owners(send_rows, "dp").reshape(fork_shape)
     incoming = jnp.arange(groups, dtype=jnp.int32) * groups + group_index
     targets = fork_child[incoming] - group_index * local_rows
     take_new = owner_index >= fork_block[incoming]

time: 138 us -> 138 us (level)
    all_to_all x1 -> x0, starting transfers between devices: 11 us -> none  [shards(): lax.all_to_all(send_rows, 'dp', split_axis=0, concat_axis=0, tiled=True)]
    all_to_all x3 -> x4, starting transfers between devices: 26.6 us -> 37.5 us  [spread_to_owners(): return lax.all_to_all(blocks, axis, 0, 0, tiled=True)]
    all_to_all x1 -> x0, waiting for transfers between devices: 4.48 us -> none  [shards(): lax.all_to_all(send_rows, 'dp', split_axis=0, concat_axis=0, tiled=True)]
    all_to_all x3 -> x4, waiting for transfers between devices: 36.9 us -> 41.4 us  [spread_to_owners(): return lax.all_to_all(blocks, axis, 0, 0, tiled=True)]
where the time goes in v4:
time: 138 us
  waiting for transfers between devices  41.4 us (30%)
  starting transfers between devices  37.5 us (27%)
  blocking collectives  26.7 us (19%)
  local copies, waits for them, and re-layouts  16 us (12%)
  other arithmetic  10.4 us (8%)
  matrix products  4.55 us (3%)
    all_to_all x4, waiting for transfers between devices, spread_to_owners(): return lax.all_to_all(blocks, axis, 0, 0, tiled=True)  41.4 us
    all_to_all x4, starting transfers between devices, spread_to_owners(): return lax.all_to_all(blocks, axis, 0, 0, tiled=True)  37.5 us
    all_to_all x1, blocking collectives, spread_to_owners(): return lax.all_to_all(blocks, axis, 0, 0, tiled=True)  26.7 us
    unnamed x39, local copies, waits for them, and re-layouts  4.8 us
  transfers between devices with their start and end apart: 4, of which 4 were waited for; matrix products, arithmetic and copies ran while one was open for 9% of the time, Pallas kernels for 0%

profile of v4, /device:TPU:1, one launch (start us, length us, event | category | flops | bytes accessed | tf_op | source)
XLA Modules:
  0.0 137.8 jit_solution(13737607455569791543)
XLA Ops:
  0.7 1.1 copy.155
  2.7 0.8 broadcast_select_fusion
  3.4 11.0 %all-to-all-start = ((bf16[8,8,2048]{2,1,0:T(8,128)(2,1)}), bf16[8,8,2048]{2,1,0:T(8,128)(2,1)S(1)}, u32[]{:S(2)}, u32[]{:S(2)}) async-start(bf16[8,8,2048]{2,1,0:T(8,128)(2,1)} %broadcast_select_fusion), calls=%async_computation | async-start | bytes 524288 | tf_op jit(solution)/shard_map/all_to_all | solution.py:13
  16.2 2.7 %add_reduce_fusion = s32[128,64]{1,0:T(8,128)S(1)} fusion(s32[128]{0:T(128)S(1)} %eq.62), kind=kOutput, calls=%fused_computation.7 | output fusion | flops 1064960 | bytes 33280 | tf_op jit(solution)/shard_map/jit(cumsum)/reduce_window_sum | solution.py:160
  20.3 4.5 %all-to-all-done = bf16[8,8,2048]{2,1,0:T(8,128)(2,1)S(1)} async-done(((bf16[8,8,2048]{2,1,0:T(8,128)(2,1)}), bf16[8,8,2048]{2,1,0:T(8,128)(2,1)S(1)}, u32[]{:S(2)}, u32[]{:S(2)}) %all-to-all-start) | async-done | bytes 262176 | tf_op jit(solution)/shard_map/all_to_all | solution.py:13
  25.0 0.8 scatter_fusion
  27.3 0.8 pad_maximum_fusion
  28.1 12.6 %all-to-all-start.1 = ((bf16[64,17,128]{2,1,0:T(8,128)(2,1)}), bf16[64,17,128]{2,1,0:T(8,128)(2,1)S(1)}, u32[]{:S(2)}, u32[]{:S(2)}) async-start(bf16[64,17,128]{2,1,0:T(8,128)(2,1)} %pad_maximum_fusion), calls=%async_computation.1 | async-start | bytes 786432 | tf_op jit(solution)/shard_map/all_to_all | solution.py:13
  43.3 0.7 constant_dynamic-slice_fusion.1
  44.8 0.8 fusion.37
  45.6 0.8 multiply_reduce_fusion.2
  46.4 9.4 %all-to-all-done.1 = bf16[64,17,128]{2,1,0:T(8,128)(2,1)S(1)} async-done(((bf16[64,17,128]{2,1,0:T(8,128)(2,1)}), bf16[64,17,128]{2,1,0:T(8,128)(2,1)S(1)}, u32[]{:S(2)}, u32[]{:S(2)}) %all-to-all-start.1) | async-done | bytes 278560 | tf_op jit(solution)/shard_map/all_to_all | solution.py:13
  56.6 0.9 fusion.5
  57.6 0.9 reshape.637
  58.4 5.6 %all-to-all-start.2 = ((bf16[64,2,512]{2,1,0:T(2,128)(2,1)}), bf16[64,2,512]{2,1,0:T(2,128)(2,1)S(1)}, u32[]{:S(2)}, u32[]{:S(2)}) async-start(bf16[64,2,512]{2,1,0:T(2,128)(2,1)} %reshape.637), calls=%async_computation.2 | async-start | bytes 262144 | tf_op jit(solution)/shard_map/all_to_all | solution.py:13
  64.3 10.9 %all-to-all-done.2 = bf16[64,2,512]{2,1,0:T(2,128)(2,1)S(1)} async-done(((bf16[64,2,512]{2,1,0:T(2,128)(2,1)}), bf16[64,2,512]{2,1,0:T(2,128)(2,1)S(1)}, u32[]{:S(2)}, u32[]{:S(2)}) %all-to-all-start.2) | async-done | bytes 131104 | tf_op jit(solution)/shard_map/all_to_all | solution.py:13
  75.5 0.8 convert_add_fusion
  76.2 0.9 gather_fusion.4
  77.6 26.7 %all_to_all.25 = bf16[512,2,128]{2,1,0:T(2,128)(2,1)S(1)} all-to-all(bf16[512,2,128]{2,1,0:T(2,128)(2,1)S(1)} %reshape.639), channel_id=1, replica_groups=mesh['dp'=8,'expert'=64] {'dp','expert'}, dimensions={0} | all-to-all | bytes 524288 | tf_op jit(solution)/shard_map/all_to_all | solution.py:13
  106.4 1.5 %fusion.11 = f32[32,128]{1,0:T(8,128)S(1)} fusion(bf16[32,4096]{1,0:T(8,128)(2,1)S(1)} %convert_element_type.158, bf16[1,4096,128]{2,1,0:T(8,128)(2,1)} %param.27), kind=kOutput, calls=%fused_computation.25 | convolution fusion | flops 33554432 | bytes 1327104 | tf_op jit(solution)/shard_map/dot_general | solution.py:180
  109.5 0.9 reshape.641
  110.4 8.4 %all-to-all-start.4 = ((bf16[512,2,128]{2,1,0:T(2,128)(2,1)}), bf16[512,2,128]{2,1,0:T(2,128)(2,1)S(1)}, u32[]{:S(2)}, u32[]{:S(2)}) async-start(bf16[512,2,128]{2,1,0:T(2,128)(2,1)} %reshape.641), calls=%async_computation.4 | async-start | bytes 524288 | tf_op jit(solution)/shard_map/all_to_all | solution.py:13
  119.7 16.7 %all-to-all-done.4 = bf16[512,2,128]{2,1,0:T(2,128)(2,1)S(1)} async-done(((bf16[512,2,128]{2,1,0:T(2,128)(2,1)}), bf16[512,2,128]{2,1,0:T(2,128)(2,1)S(1)}, u32[]{:S(2)}, u32[]{:S(2)}) %all-to-all-start.4) | async-done | bytes 262176 | tf_op jit(solution)/shard_map/all_to_all | solution.py:13
  137.0 0.8 fusion.7
  (109 shorter events, 15.8 us)
Async XLA Ops:
  0.6 107.3 %copy-start = (bf16[1,128,4096]{2,1,0:T(8,128)(2,1)S(1)}, bf16[1,128,4096]{2,1,0:T(8,128)(2,1)}, u32[]{:S(2)}) copy-start(bf16[1,128,4096]{2,1,0:T(8,128)(2,1)} %param.29) | copy-start | bytes 3145732
  0.6 1.1 copy-start.12
  0.7 1.9 %copy-start.1 = (s32[64]{0:T(128)S(1)}, s32[64]{0:T(128)}, u32[]{:S(2)}) copy-start(s32[64]{0:T(128)} %param.22) | copy-start | bytes 772
  1.9 12.6 %copy-start.10 = (s32[128,8]{0,1:T(8,128)S(1)}, s32[128,8]{0,1:T(8,128)}, u32[]{:S(2)}) copy-start(s32[128,8]{0,1:T(8,128)} %param.25) | copy-start | bytes 12292
  2.5 13.0 %copy-start.2 = (s32[64]{0:T(128)S(1)}, s32[64]{0:T(128)}, u32[]{:S(2)}) copy-start(s32[64]{0:T(128)} %param.21) | copy-start | bytes 772
  3.4 16.2 %copy-start.7 = (bf16[16,8192]{1,0:T(8,128)(2,1)S(1)}, bf16[16,8192]{1,0:T(8,128)(2,1)}, u32[]{:S(2)}) copy-start(bf16[16,8192]{1,0:T(8,128)(2,1)} %param.16) | copy-start | bytes 786436
  3.4 21.4 %all-to-all-start = ((bf16[8,8,2048]{2,1,0:T(8,128)(2,1)}), bf16[8,8,2048]{2,1,0:T(8,128)(2,1)S(1)}, u32[]{:S(2)}, u32[]{:S(2)}) async-start(bf16[8,8,2048]{2,1,0:T(8,128)(2,1)} %broadcast_select_fusion), calls=%async_computation | async-start | bytes 524288 | tf_op jit(solution)/shard_map/all_to_all | solution.py:13
  14.8 5.4 %copy-start.13 = (s32[16]{0:T(128)S(1)}, s32[16]{0:T(128)}, u32[]{:S(2)}) copy-start(s32[16]{0:T(128)} %param.19) | copy-start | bytes 196
  14.8 5.5 %copy-start.9 = (bf16[16,1024]{1,0:T(8,128)(2,1)S(1)}, bf16[16,1024]{1,0:T(8,128)(2,1)}, u32[]{:S(2)}) copy-start(bf16[16,1024]{1,0:T(8,128)(2,1)} %param.17) | copy-start | bytes 98308
  18.9 0.7 copy-start.5
  27.1 15.5 %copy-start.3 = (bf16[128,4096]{1,0:T(8,128)(2,1)S(1)}, bf16[128,4096]{1,0:T(8,128)(2,1)}, u32[]{:S(2)}) copy-start(bf16[128,4096]{1,0:T(8,128)(2,1)} %param.23) | copy-start | bytes 3145732
  28.1 27.6 %all-to-all-start.1 = ((bf16[64,17,128]{2,1,0:T(8,128)(2,1)}), bf16[64,17,128]{2,1,0:T(8,128)(2,1)S(1)}, u32[]{:S(2)}, u32[]{:S(2)}) async-start(bf16[64,17,128]{2,1,0:T(8,128)(2,1)} %pad_maximum_fusion), calls=%async_computation.1 | async-start | bytes 786432 | tf_op jit(solution)/shard_map/all_to_all | solution.py:13
  57.6 19.5 %copy-start.8 = (pred[64,4]{1,0:T(8,128)(4,1)S(1)}, pred[64,4]{1,0:T(8,128)(4,1)}, u32[]{:S(2)}) copy-start(pred[64,4]{1,0:T(8,128)(4,1)} %copy.106) | copy-start | bytes 772
  58.4 16.7 %all-to-all-start.2 = ((bf16[64,2,512]{2,1,0:T(2,128)(2,1)}), bf16[64,2,512]{2,1,0:T(2,128)(2,1)S(1)}, u32[]{:S(2)}, u32[]{:S(2)}) async-start(bf16[64,2,512]{2,1,0:T(2,128)(2,1)} %reshape.637), calls=%async_computation.2 | async-start | bytes 262144 | tf_op jit(solution)/shard_map/all_to_all | solution.py:13
  105.9 2.0 %copy-start.4 = (bf16[1,4096,128]{2,1,0:T(8,128)(2,1)S(1)}, bf16[1,4096,128]{2,1,0:T(8,128)(2,1)}, u32[]{:S(2)}) copy-start(bf16[1,4096,128]{2,1,0:T(8,128)(2,1)} %param.28) | copy-start | bytes 3145732
  109.0 9.8 %copy-start.11 = (f32[128,8]{0,1:T(8,128)S(1)}, f32[128,8]{0,1:T(8,128)}, u32[]{:S(2)}) copy-start(f32[128,8]{0,1:T(8,128)} %param.26) | copy-start | bytes 12292
  109.1 9.9 %copy-start.6 = (s32[128,64]{1,0:T(8,128)S(1)}, s32[128,64]{1,0:T(8,128)}, u32[]{:S(2)}) copy-start(s32[128,64]{1,0:T(8,128)} %copy-done.5) | copy-start | bytes 98308
  110.4 26.0 %all-to-all-start.4 = ((bf16[512,2,128]{2,1,0:T(2,128)(2,1)}), bf16[512,2,128]{2,1,0:T(2,128)(2,1)S(1)}, u32[]{:S(2)}, u32[]{:S(2)}) async-start(bf16[512,2,128]{2,1,0:T(2,128)(2,1)} %reshape.641), calls=%async_computation.4 | async-start | bytes 524288 | tf_op jit(solution)/shard_map/all_to_all | solution.py:13

commit v5 on v4

--- a/solution.py
+++ b/solution.py
@@ -54,12 +54,7 @@
         lax.dynamic_slice_in_dim(fork_parent, group_index * groups, groups)
         - group_index * local_rows
     )
-    out_blocks = lax.dynamic_slice_in_dim(fork_block, group_index * groups, groups)
-    send_rows = jnp.where(
-        (owner_index >= out_blocks)[:, None, None],
-        kv_cache[outgoing],
-        jnp.zeros((), kv_cache.dtype),
-    )
+    send_rows = kv_cache[outgoing]
     fork_shape = send_rows.shape
     send_rows = send_rows.reshape(fork_shape[0], fork_shape[1] // 2, 2 * fork_shape[2])
     arrived = spread_to_owners(send_rows, "dp").reshape(fork_shape)
@@ -171,19 +166,33 @@
     slot_cols = jnp.broadcast_to(slot_cols[None], (groups,) + slot_cols.shape)
     slot_cols = slot_cols.reshape(groups * experts_total, capacity, columns)
     rows_in = spread_to_owners(slot_cols, ("dp", "expert"))
-    rows_in = rows_in.reshape(groups, owners, capacity, columns).transpose(0, 2, 1, 3)
-    stream_rows = rows_in.reshape(groups * capacity, model_width).astype(jnp.float32)
+    rows_in = rows_in.reshape(groups, owners, capacity, columns).astype(jnp.float32)
     inverse = lax.rsqrt(
-        jnp.sum(stream_rows * stream_rows, axis=1, keepdims=True) / model_width + 1e-06
-    )
-    piece = (stream_rows * inverse).astype(jnp.bfloat16)
-    gate_proj = jnp.dot(piece, w_gate[0], preferred_element_type=jnp.float32)
-    up_proj = jnp.dot(piece, w_up[0], preferred_element_type=jnp.float32)
+        jnp.sum(rows_in * rows_in, axis=(1, 3), keepdims=True) / model_width + 1e-06
+    )
+    piece = (rows_in * inverse).astype(jnp.bfloat16)
+    hidden_width = w_gate.shape[2]
+    gate_proj = jnp.einsum(
+        "gosc,ocf->gsf",
+        piece,
+        w_gate[0].reshape(owners, columns, hidden_width),
+        preferred_element_type=jnp.float32,
+    )
+    up_proj = jnp.einsum(
+        "gosc,ocf->gsf",
+        piece,
+        w_up[0].reshape(owners, columns, hidden_width),
+        preferred_element_type=jnp.float32,
+    )
     hidden = (jax.nn.silu(gate_proj) * up_proj).astype(jnp.bfloat16)
-    outputs = jnp.dot(hidden, w_down[0], preferred_element_type=jnp.float32)
-
-    out_blocks = outputs.astype(jnp.bfloat16).reshape(groups, capacity, owners, columns)
-    out_blocks = out_blocks.transpose(0, 2, 1, 3).reshape(groups * owners, capacity, columns)
+    outputs = jnp.einsum(
+        "gsf,foc->gosc",
+        hidden,
+        w_down[0].reshape(hidden_width, owners, columns),
+        preferred_element_type=jnp.float32,
+    )
+
+    out_blocks = outputs.astype(jnp.bfloat16).reshape(groups * owners, capacity, columns)
     partials = spread_to_owners(out_blocks, ("dp", "expert"))
     partials = partials.reshape(groups, experts_total, capacity, columns)
     summed = jnp.sum(partials.astype(jnp.float32), axis=0)

time: 138 us -> 141 us (1.022)
  blocking collectives: 26.7 us -> 0 us
  waiting for transfers between devices: 41.4 us -> 63.5 us
  starting transfers between devices: 37.5 us -> 46.2 us
  matrix products: 4.55 us -> 8.7 us
  other arithmetic: 10.4 us -> 7.71 us
  local copies, waits for them, and re-layouts: 16 us -> 13.4 us
    all_to_all x1 -> x0, blocking collectives: 26.7 us -> none  [spread_to_owners(): return lax.all_to_all(blocks, axis, 0, 0, tiled=True)]
    all_to_all x4 -> x5, waiting for transfers between devices: 41.4 us -> 63.5 us  [spread_to_owners(): return lax.all_to_all(blocks, axis, 0, 0, tiled=True)]
    all_to_all x4 -> x5, starting transfers between devices: 37.5 us -> 46.2 us  [spread_to_owners(): return lax.all_to_all(blocks, axis, 0, 0, tiled=True)]
    dot_general x2, matrix products: 2.04 us -> 6.18 us  [the longest x1 3.59 us: shards(): jnp.einsum('gsf,foc->gosc', hidden, w_down[0].reshape(hidden_width, owner...]
    unnamed x39 -> x33, local copies, waits for them, and re-layouts: 4.8 us -> 6.2 us
  transfers between devices with their start and end apart: 4 -> 5, of which waited for: 4 -> 5; matrix products, arithmetic and copies ran while one was open for 9% -> 6% of each run, Pallas kernels for 0% -> 0%
where the time goes in v5:
time: 141 us
  waiting for transfers between devices  63.5 us (45%)
  starting transfers between devices  46.2 us (33%)
  local copies, waits for them, and re-layouts  13.4 us (10%)
  matrix products  8.7 us (6%)
  other arithmetic  7.71 us (5%)
    all_to_all x5, waiting for transfers between devices, spread_to_owners(): return lax.all_to_all(blocks, axis, 0, 0, tiled=True)  63.5 us
    all_to_all x5, starting transfers between devices, spread_to_owners(): return lax.all_to_all(blocks, axis, 0, 0, tiled=True)  46.2 us
    unnamed x33, local copies, waits for them, and re-layouts  6.2 us
    dot_general x1, matrix products, shards(): jnp.einsum('gsf,foc->gosc', hidden, w_down[0].reshape(hidden_width, owner...  3.59 us
  transfers between devices with their start and end apart: 5, of which 5 were waited for; matrix products, arithmetic and copies ran while one was open for 6% of the time, Pallas kernels for 0%

profile of v5, /device:TPU:1, one launch (start us, length us, event | category | flops | bytes accessed | tf_op | source)
XLA Modules:
  0.0 140.6 jit_solution(12607885933002389271)
XLA Ops:
  0.7 1.1 copy.147
  2.4 0.8 reshape.486
  3.2 11.0 %all-to-all-start = ((bf16[8,8,2048]{2,1,0:T(8,128)(2,1)}), bf16[8,8,2048]{2,1,0:T(8,128)(2,1)S(1)}, u32[]{:S(2)}, u32[]{:S(2)}) async-start(bf16[8,8,2048]{2,1,0:T(8,128)(2,1)} %reshape.486), calls=%async_computation | async-start | bytes 524288 | tf_op jit(solution)/shard_map/all_to_all | solution.py:13
  15.9 2.7 %add_reduce_fusion = s32[128,64]{1,0:T(8,128)S(1)} fusion(s32[128]{0:T(128)S(1)} %eq.62), kind=kOutput, calls=%fused_computation.6 | output fusion | flops 1064960 | bytes 33280 | tf_op jit(solution)/shard_map/jit(cumsum)/reduce_window_sum | solution.py:155
  19.5 5.1 %all-to-all-done = bf16[8,8,2048]{2,1,0:T(8,128)(2,1)S(1)} async-done(((bf16[8,8,2048]{2,1,0:T(8,128)(2,1)}), bf16[8,8,2048]{2,1,0:T(8,128)(2,1)S(1)}, u32[]{:S(2)}, u32[]{:S(2)}) %all-to-all-start) | async-done | bytes 262176 | tf_op jit(solution)/shard_map/all_to_all | solution.py:13
  24.7 0.8 scatter_fusion
  27.1 0.8 pad_maximum_fusion
  27.8 12.6 %all-to-all-start.1 = ((bf16[64,17,128]{2,1,0:T(8,128)(2,1)}), bf16[64,17,128]{2,1,0:T(8,128)(2,1)S(1)}, u32[]{:S(2)}, u32[]{:S(2)}) async-start(bf16[64,17,128]{2,1,0:T(8,128)(2,1)} %pad_maximum_fusion), calls=%async_computation.1 | async-start | bytes 786432 | tf_op jit(solution)/shard_map/all_to_all | solution.py:13
  41.5 14.0 %all-to-all-done.1 = bf16[64,17,128]{2,1,0:T(8,128)(2,1)S(1)} async-done(((bf16[64,17,128]{2,1,0:T(8,128)(2,1)}), bf16[64,17,128]{2,1,0:T(8,128)(2,1)S(1)}, u32[]{:S(2)}, u32[]{:S(2)}) %all-to-all-start.1) | async-done | bytes 278560 | tf_op jit(solution)/shard_map/all_to_all | solution.py:13
  56.4 0.9 fusion.6
  57.3 0.9 reshape.625
  58.2 5.6 %all-to-all-start.2 = ((bf16[64,2,512]{2,1,0:T(2,128)(2,1)}), bf16[64,2,512]{2,1,0:T(2,128)(2,1)S(1)}, u32[]{:S(2)}, u32[]{:S(2)}) async-start(bf16[64,2,512]{2,1,0:T(2,128)(2,1)} %reshape.625), calls=%async_computation.2 | async-start | bytes 262144 | tf_op jit(solution)/shard_map/all_to_all | solution.py:13
  64.0 10.9 %all-to-all-done.2 = bf16[64,2,512]{2,1,0:T(2,128)(2,1)S(1)} async-done(((bf16[64,2,512]{2,1,0:T(2,128)(2,1)}), bf16[64,2,512]{2,1,0:T(2,128)(2,1)S(1)}, u32[]{:S(2)}, u32[]{:S(2)}) %all-to-all-start.2) | async-done | bytes 131104 | tf_op jit(solution)/shard_map/all_to_all | solution.py:13
  75.2 0.8 convert_add_fusion
  76.0 0.9 gather_fusion.4
  77.1 1.0 reshape.627
  78.1 8.6 %all-to-all-start.3 = ((bf16[512,2,128]{2,1,0:T(2,128)(2,1)}), bf16[512,2,128]{2,1,0:T(2,128)(2,1)S(1)}, u32[]{:S(2)}, u32[]{:S(2)}) async-start(bf16[512,2,128]{2,1,0:T(2,128)(2,1)} %reshape.627), calls=%async_computation.3 | async-start | bytes 524288 | tf_op jit(solution)/shard_map/all_to_all | solution.py:13
  87.4 16.9 %all-to-all-done.3 = bf16[512,2,128]{2,1,0:T(2,128)(2,1)S(1)} async-done(((bf16[512,2,128]{2,1,0:T(2,128)(2,1)}), bf16[512,2,128]{2,1,0:T(2,128)(2,1)S(1)}, u32[]{:S(2)}, u32[]{:S(2)}) %all-to-all-start.3) | async-done | bytes 262176 | tf_op jit(solution)/shard_map/all_to_all | solution.py:13
  105.7 2.6 %convolution_bitcast_fusion.1 = f32[8,4,128]{2,0,1:T(8,128)S(1)} fusion(bf16[64,64,128]{2,1,0:T(8,128)(2,1)} %bitcast.168, f32[8,64,4,64]{1,0,3,2:T(8,128)S(1)} %copy.83, f32[8,4]{0,1:T(4,128)S(1)} %add_rsqrt_fusion), kind=kOutput, calls=%fused_computation.20 | convolution fusion | flops 33816576 | bytes 1589376 | tf_op jit(solution)/shard_map/gosc,ocf->gsf/dot_general | solution.py:175
  108.3 3.6 %fusion.3 = bf16[8,64,4,64]{3,0,1,2:T(8,128)(2,1)S(1)} fusion(bf16[128,64,64,1]{0,2,1,3:T(8,128)(2,1)S(1)} %bitcast.162, bf16[64,64,128]{2,1,0:T(8,128)(2,1)} %bitcast.167, f32[8,64,4,64]{1,0,3,2:T(8,128)S(1)} %copy.83, f32[8,4]{0,1:T(4,128)S(1)} %add_rsqrt_fusion, f32[8,4,128]{2,0,1:T(8,128)S(1)} %convolution_bitcast_fusion.1), kind=kOutput, calls=%fused_computation.12 | convolution fusion | flops 67526656 | bytes 2900096 | tf_op jit(solution)/shard_map/gsf,foc->gosc/dot_general | solution.py:188
  112.3 1.0 reshape.629
  113.3 8.4 %all-to-all-start.4 = ((bf16[512,2,128]{2,1,0:T(2,128)(2,1)}), bf16[512,2,128]{2,1,0:T(2,128)(2,1)S(1)}, u32[]{:S(2)}, u32[]{:S(2)}) async-start(bf16[512,2,128]{2,1,0:T(2,128)(2,1)} %reshape.629), calls=%async_computation.4 | async-start | bytes 524288 | tf_op jit(solution)/shard_map/all_to_all | solution.py:13
  122.6 16.7 %all-to-all-done.4 = bf16[512,2,128]{2,1,0:T(2,128)(2,1)S(1)} async-done(((bf16[512,2,128]{2,1,0:T(2,128)(2,1)}), bf16[512,2,128]{2,1,0:T(2,128)(2,1)S(1)}, u32[]{:S(2)}, u32[]{:S(2)}) %all-to-all-start.4) | async-done | bytes 262176 | tf_op jit(solution)/shard_map/all_to_all | solution.py:13
  139.8 0.8 fusion.10
  (98 shorter events, 11.4 us)
Async XLA Ops:
  0.6 13.5 %copy-start = (s32[128,8]{0,1:T(8,128)S(1)}, s32[128,8]{0,1:T(8,128)}, u32[]{:S(2)}) copy-start(s32[128,8]{0,1:T(8,128)} %param.25) | copy-start | bytes 12292
  0.6 1.1 copy-start.8
  1.7 12.8 %copy-start.1 = (s32[64]{0:T(128)S(1)}, s32[64]{0:T(128)}, u32[]{:S(2)}) copy-start(s32[64]{0:T(128)} %param.22) | copy-start | bytes 772
  1.8 13.4 %copy-start.2 = (s32[64]{0:T(128)S(1)}, s32[64]{0:T(128)}, u32[]{:S(2)}) copy-start(s32[64]{0:T(128)} %param.21) | copy-start | bytes 772
  3.2 15.6 %copy-start.5 = (bf16[16,8192]{1,0:T(8,128)(2,1)S(1)}, bf16[16,8192]{1,0:T(8,128)(2,1)}, u32[]{:S(2)}) copy-start(bf16[16,8192]{1,0:T(8,128)(2,1)} %param.16) | copy-start | bytes 786436
  3.2 21.4 %all-to-all-start = ((bf16[8,8,2048]{2,1,0:T(8,128)(2,1)}), bf16[8,8,2048]{2,1,0:T(8,128)(2,1)S(1)}, u32[]{:S(2)}, u32[]{:S(2)}) async-start(bf16[8,8,2048]{2,1,0:T(8,128)(2,1)} %reshape.486), calls=%async_computation | async-start | bytes 524288 | tf_op jit(solution)/shard_map/all_to_all | solution.py:13
  14.5 4.8 %copy-start.9 = (s32[16]{0:T(128)S(1)}, s32[16]{0:T(128)}, u32[]{:S(2)}) copy-start(s32[16]{0:T(128)} %param.19) | copy-start | bytes 196
  14.5 4.9 %copy-start.6 = (bf16[16,1024]{1,0:T(8,128)(2,1)S(1)}, bf16[16,1024]{1,0:T(8,128)(2,1)}, u32[]{:S(2)}) copy-start(bf16[16,1024]{1,0:T(8,128)(2,1)} %param.17) | copy-start | bytes 98308
  26.9 13.7 %copy-start.3 = (bf16[128,4096]{1,0:T(8,128)(2,1)S(1)}, bf16[128,4096]{1,0:T(8,128)(2,1)}, u32[]{:S(2)}) copy-start(bf16[128,4096]{1,0:T(8,128)(2,1)} %param.23) | copy-start | bytes 3145732
  27.8 27.6 %all-to-all-start.1 = ((bf16[64,17,128]{2,1,0:T(8,128)(2,1)}), bf16[64,17,128]{2,1,0:T(8,128)(2,1)S(1)}, u32[]{:S(2)}, u32[]{:S(2)}) async-start(bf16[64,17,128]{2,1,0:T(8,128)(2,1)} %pad_maximum_fusion), calls=%async_computation.1 | async-start | bytes 786432 | tf_op jit(solution)/shard_map/all_to_all | solution.py:13
  58.2 16.7 %all-to-all-start.2 = ((bf16[64,2,512]{2,1,0:T(2,128)(2,1)}), bf16[64,2,512]{2,1,0:T(2,128)(2,1)S(1)}, u32[]{:S(2)}, u32[]{:S(2)}) async-start(bf16[64,2,512]{2,1,0:T(2,128)(2,1)} %reshape.625), calls=%async_computation.2 | async-start | bytes 262144 | tf_op jit(solution)/shard_map/all_to_all | solution.py:13
  76.8 9.9 %copy-start.4 = (bf16[1,128,4096]{2,1,0:T(8,128)(2,1)S(1)}, bf16[1,128,4096]{2,1,0:T(8,128)(2,1)}, u32[]{:S(2)}) copy-start(bf16[1,128,4096]{2,1,0:T(8,128)(2,1)} %param.29) | copy-start | bytes 3145732
  78.1 26.2 %all-to-all-start.3 = ((bf16[512,2,128]{2,1,0:T(2,128)(2,1)}), bf16[512,2,128]{2,1,0:T(2,128)(2,1)S(1)}, u32[]{:S(2)}, u32[]{:S(2)}) async-start(bf16[512,2,128]{2,1,0:T(2,128)(2,1)} %reshape.627), calls=%async_computation.3 | async-start | bytes 524288 | tf_op jit(solution)/shard_map/all_to_all | solution.py:13
  111.9 9.8 %copy-start.7 = (f32[128,8]{0,1:T(8,128)S(1)}, f32[128,8]{0,1:T(8,128)}, u32[]{:S(2)}) copy-start(f32[128,8]{0,1:T(8,128)} %param.26) | copy-start | bytes 12292
  113.3 26.0 %all-to-all-start.4 = ((bf16[512,2,128]{2,1,0:T(2,128)(2,1)}), bf16[512,2,128]{2,1,0:T(2,128)(2,1)S(1)}, u32[]{:S(2)}, u32[]{:S(2)}) async-start(bf16[512,2,128]{2,1,0:T(2,128)(2,1)} %reshape.629), calls=%async_computation.4 | async-start | bytes 524288 | tf_op jit(solution)/shard_map/all_to_all | solution.py:13

commit v6 on v4

--- a/solution.py
+++ b/solution.py
@@ -54,12 +54,7 @@
         lax.dynamic_slice_in_dim(fork_parent, group_index * groups, groups)
         - group_index * local_rows
     )
-    out_blocks = lax.dynamic_slice_in_dim(fork_block, group_index * groups, groups)
-    send_rows = jnp.where(
-        (owner_index >= out_blocks)[:, None, None],
-        kv_cache[outgoing],
-        jnp.zeros((), kv_cache.dtype),
-    )
+    send_rows = kv_cache[outgoing]
     fork_shape = send_rows.shape
     send_rows = send_rows.reshape(fork_shape[0], fork_shape[1] // 2, 2 * fork_shape[2])
     arrived = spread_to_owners(send_rows, "dp").reshape(fork_shape)
@@ -98,15 +93,12 @@
     stat_width = -(-6 * head_block // HD) * HD
     stat_parts = jnp.pad(stat_parts, ((0, 0), (0, stat_width - 6 * head_block)))
     packed = jnp.concatenate(
-        [
-            send_out.astype(jnp.bfloat16).reshape(owners, head_block, HD),
-            stat_parts.reshape(owners, stat_width // HD, HD),
-        ],
-        axis=1,
-    )
-    got = spread_to_owners(packed, "expert")
-    got_out = got[:, :head_block].astype(jnp.float32).reshape(owners, local_rows, own_heads, HD)
-    got_stats = got[:, head_block:].reshape(owners, stat_width)[:, : 6 * head_block]
+        [send_out.astype(jnp.bfloat16).reshape(owners, head_block * HD), stat_parts], axis=1
+    )
+    got = spread_to_owners(packed[:, None], "expert")[:, 0]
+    got_out = got[:, : head_block * HD].astype(jnp.float32)
+    got_out = got_out.reshape(owners, local_rows, own_heads, HD)
+    got_stats = got[:, head_block * HD : head_block * HD + 6 * head_block]
     got_stats = got_stats.reshape(owners, 3, 2 * head_block).astype(jnp.float32)
     got_stats = (got_stats[:, 0] + got_stats[:, 1]) + got_stats[:, 2]
     got_stats = got_stats.reshape(owners, 2, local_rows, own_heads)

time: 138 us -> 139 us (level)
  local copies, waits for them, and re-layouts: 16 us -> 18.5 us
  other arithmetic: 10.4 us -> 8.78 us
  transfers between devices with their start and end apart: 4 -> 4, of which waited for: 4 -> 4; matrix products, arithmetic and copies ran while one was open for 9% -> 8% of each run, Pallas kernels for 0% -> 0%
where the time goes in v6:
time: 139 us; the launch traced here: 138 us
  waiting for transfers between devices  41.6 us (30%)
  starting transfers between devices  36.8 us (26%)
  blocking collectives  26.7 us (19%)
  local copies, waits for them, and re-layouts  18.5 us (13%)
  other arithmetic  8.78 us (6%)
  matrix products  4.58 us (3%)
    all_to_all x4, waiting for transfers between devices, spread_to_owners(): return lax.all_to_all(blocks, axis, 0, 0, tiled=True)  41.6 us
    all_to_all x4, starting transfers between devices, spread_to_owners(): return lax.all_to_all(blocks, axis, 0, 0, tiled=True)  36.8 us
    all_to_all x1, blocking collectives, spread_to_owners(): return lax.all_to_all(blocks, axis, 0, 0, tiled=True)  26.7 us
    unnamed x39, local copies, waits for them, and re-layouts  6.08 us
  transfers between devices with their start and end apart: 4, of which 4 were waited for; matrix products, arithmetic and copies ran while one was open for 8% of the time, Pallas kernels for 0%

profile of v6, /device:TPU:1, one launch (start us, length us, event | category | flops | bytes accessed | tf_op | source)
XLA Modules:
  0.0 138.1 jit_solution(13092690285896691156)
XLA Ops:
  0.7 1.1 copy.160
  2.5 0.8 reshape.504
  3.3 11.0 %all-to-all-start = ((bf16[8,8,2048]{2,1,0:T(8,128)(2,1)}), bf16[8,8,2048]{2,1,0:T(8,128)(2,1)S(1)}, u32[]{:S(2)}, u32[]{:S(2)}) async-start(bf16[8,8,2048]{2,1,0:T(8,128)(2,1)} %reshape.504), calls=%async_computation | async-start | bytes 524288 | tf_op jit(solution)/shard_map/all_to_all | solution.py:13
  15.3 2.7 %add_reduce_fusion = s32[128,64]{1,0:T(8,128)S(1)} fusion(s32[128]{0:T(128)S(1)} %eq.62), kind=kOutput, calls=%fused_computation.7 | output fusion | flops 1064960 | bytes 33280 | tf_op jit(solution)/shard_map/jit(cumsum)/reduce_window_sum | solution.py:152
  21.3 3.3 %all-to-all-done = bf16[8,8,2048]{2,1,0:T(8,128)(2,1)S(1)} async-done(((bf16[8,8,2048]{2,1,0:T(8,128)(2,1)}), bf16[8,8,2048]{2,1,0:T(8,128)(2,1)S(1)}, u32[]{:S(2)}, u32[]{:S(2)}) %all-to-all-start) | async-done | bytes 262176 | tf_op jit(solution)/shard_map/all_to_all | solution.py:13
  27.7 0.8 reduce.10
  28.5 1.0 reshape.636
  29.5 12.6 %all-to-all-start.1 = ((bf16[64,2,1088]{2,1,0:T(2,128)(2,1)}), bf16[64,2,1088]{2,1,0:T(2,128)(2,1)S(1)}, u32[]{:S(2)}, u32[]{:S(2)}) async-start(bf16[64,2,1088]{2,1,0:T(2,128)(2,1)} %reshape.636), calls=%async_computation.1 | async-start | bytes 589824 | tf_op jit(solution)/shard_map/all_to_all | solution.py:13
  43.5 0.8 constant_dynamic-slice_fusion
  44.2 0.8 fusion.41
  45.1 10.7 %all-to-all-done.1 = bf16[64,2,1088]{2,1,0:T(2,128)(2,1)S(1)} async-done(((bf16[64,2,1088]{2,1,0:T(2,128)(2,1)}), bf16[64,2,1088]{2,1,0:T(2,128)(2,1)S(1)}, u32[]{:S(2)}, u32[]{:S(2)}) %all-to-all-start.1) | async-done | bytes 278560 | tf_op jit(solution)/shard_map/all_to_all | solution.py:13
  56.1 0.8 copy.103
  57.7 0.9 fusion.5
  58.7 0.9 reshape.638
  59.5 4.8 %all-to-all-start.2 = ((bf16[64,2,512]{2,1,0:T(2,128)(2,1)}), bf16[64,2,512]{2,1,0:T(2,128)(2,1)S(1)}, u32[]{:S(2)}, u32[]{:S(2)}) async-start(bf16[64,2,512]{2,1,0:T(2,128)(2,1)} %reshape.638), calls=%async_computation.2 | async-start | bytes 262144 | tf_op jit(solution)/shard_map/all_to_all | solution.py:13
  64.6 10.9 %all-to-all-done.2 = bf16[64,2,512]{2,1,0:T(2,128)(2,1)S(1)} async-done(((bf16[64,2,512]{2,1,0:T(2,128)(2,1)}), bf16[64,2,512]{2,1,0:T(2,128)(2,1)S(1)}, u32[]{:S(2)}, u32[]{:S(2)}) %all-to-all-start.2) | async-done | bytes 131104 | tf_op jit(solution)/shard_map/all_to_all | solution.py:13
  75.8 0.8 convert_add_fusion
  76.6 0.9 gather_fusion.4
  78.0 26.7 %all_to_all.25 = bf16[512,2,128]{2,1,0:T(2,128)(2,1)S(1)} all-to-all(bf16[512,2,128]{2,1,0:T(2,128)(2,1)S(1)} %reshape.640), channel_id=1, replica_groups=mesh['dp'=8,'expert'=64] {'dp','expert'}, dimensions={0} | all-to-all | bytes 524288 | tf_op jit(solution)/shard_map/all_to_all | solution.py:13
  106.8 1.5 %fusion.11 = f32[32,128]{1,0:T(8,128)S(1)} fusion(bf16[32,4096]{1,0:T(8,128)(2,1)S(1)} %convert_element_type.158, bf16[1,4096,128]{2,1,0:T(8,128)(2,1)} %param.27), kind=kOutput, calls=%fused_computation.25 | convolution fusion | flops 33554432 | bytes 1327104 | tf_op jit(solution)/shard_map/dot_general | solution.py:172
  109.8 0.9 reshape.642
  110.8 8.4 %all-to-all-start.4 = ((bf16[512,2,128]{2,1,0:T(2,128)(2,1)}), bf16[512,2,128]{2,1,0:T(2,128)(2,1)S(1)}, u32[]{:S(2)}, u32[]{:S(2)}) async-start(bf16[512,2,128]{2,1,0:T(2,128)(2,1)} %reshape.642), calls=%async_computation.4 | async-start | bytes 524288 | tf_op jit(solution)/shard_map/all_to_all | solution.py:13
  120.1 16.7 %all-to-all-done.4 = bf16[512,2,128]{2,1,0:T(2,128)(2,1)S(1)} async-done(((bf16[512,2,128]{2,1,0:T(2,128)(2,1)}), bf16[512,2,128]{2,1,0:T(2,128)(2,1)S(1)}, u32[]{:S(2)}, u32[]{:S(2)}) %all-to-all-start.4) | async-done | bytes 262176 | tf_op jit(solution)/shard_map/all_to_all | solution.py:13
  137.3 0.8 fusion.7
  (106 shorter events, 16.4 us)
Async XLA Ops:
  0.6 107.7 %copy-start = (bf16[1,128,4096]{2,1,0:T(8,128)(2,1)S(1)}, bf16[1,128,4096]{2,1,0:T(8,128)(2,1)}, u32[]{:S(2)}) copy-start(bf16[1,128,4096]{2,1,0:T(8,128)(2,1)} %param.29) | copy-start | bytes 3145732
  0.6 1.2 copy-start.11
  1.8 12.5 %copy-start.9 = (s32[128,8]{0,1:T(8,128)S(1)}, s32[128,8]{0,1:T(8,128)}, u32[]{:S(2)}) copy-start(s32[128,8]{0,1:T(8,128)} %param.25) | copy-start | bytes 12292
  1.8 12.8 %copy-start.1 = (s32[64]{0:T(128)S(1)}, s32[64]{0:T(128)}, u32[]{:S(2)}) copy-start(s32[64]{0:T(128)} %param.21) | copy-start | bytes 772
  1.9 13.4 %copy-start.7 = (bf16[16,1024]{1,0:T(8,128)(2,1)S(1)}, bf16[16,1024]{1,0:T(8,128)(2,1)}, u32[]{:S(2)}) copy-start(bf16[16,1024]{1,0:T(8,128)(2,1)} %param.17) | copy-start | bytes 98308
  2.5 16.2 %copy-start.2 = (s32[64]{0:T(128)S(1)}, s32[64]{0:T(128)}, u32[]{:S(2)}) copy-start(s32[64]{0:T(128)} %param.22) | copy-start | bytes 772
  3.3 17.3 %copy-start.5 = (bf16[16,8192]{1,0:T(8,128)(2,1)S(1)}, bf16[16,8192]{1,0:T(8,128)(2,1)}, u32[]{:S(2)}) copy-start(bf16[16,8192]{1,0:T(8,128)(2,1)} %param.16) | copy-start | bytes 786436
  3.3 21.4 %all-to-all-start = ((bf16[8,8,2048]{2,1,0:T(8,128)(2,1)}), bf16[8,8,2048]{2,1,0:T(8,128)(2,1)S(1)}, u32[]{:S(2)}, u32[]{:S(2)}) async-start(bf16[8,8,2048]{2,1,0:T(8,128)(2,1)} %reshape.504), calls=%async_computation | async-start | bytes 524288 | tf_op jit(solution)/shard_map/all_to_all | solution.py:13
  15.3 5.9 %copy-start.12 = (s32[16]{0:T(128)S(1)}, s32[16]{0:T(128)}, u32[]{:S(2)}) copy-start(s32[16]{0:T(128)} %param.19) | copy-start | bytes 196
  27.2 14.9 %copy-start.8 = (s32[64,4]{0,1:T(4,128)S(1)}, s32[64,4]{0,1:T(4,128)}, u32[]{:S(2)}) copy-start(s32[64,4]{0,1:T(4,128)} %get-tuple-element.14) | copy-start | bytes 3076
  27.2 15.6 %copy-start.3 = (bf16[128,4096]{1,0:T(8,128)(2,1)S(1)}, bf16[128,4096]{1,0:T(8,128)(2,1)}, u32[]{:S(2)}) copy-start(bf16[128,4096]{1,0:T(8,128)(2,1)} %param.23) | copy-start | bytes 3145732
  29.5 26.3 %all-to-all-start.1 = ((bf16[64,2,1088]{2,1,0:T(2,128)(2,1)}), bf16[64,2,1088]{2,1,0:T(2,128)(2,1)S(1)}, u32[]{:S(2)}, u32[]{:S(2)}) async-start(bf16[64,2,1088]{2,1,0:T(2,128)(2,1)} %reshape.636), calls=%async_computation.1 | async-start | bytes 589824 | tf_op jit(solution)/shard_map/all_to_all | solution.py:13
  58.7 18.8 %copy-start.6 = (pred[64,4]{1,0:T(8,128)(4,1)S(1)}, pred[64,4]{1,0:T(8,128)(4,1)}, u32[]{:S(2)}) copy-start(pred[64,4]{1,0:T(8,128)(4,1)} %copy.110) | copy-start | bytes 772
  59.5 16.0 %all-to-all-start.2 = ((bf16[64,2,512]{2,1,0:T(2,128)(2,1)}), bf16[64,2,512]{2,1,0:T(2,128)(2,1)S(1)}, u32[]{:S(2)}, u32[]{:S(2)}) async-start(bf16[64,2,512]{2,1,0:T(2,128)(2,1)} %reshape.638), calls=%async_computation.2 | async-start | bytes 262144 | tf_op jit(solution)/shard_map/all_to_all | solution.py:13
  106.3 2.0 %copy-start.4 = (bf16[1,4096,128]{2,1,0:T(8,128)(2,1)S(1)}, bf16[1,4096,128]{2,1,0:T(8,128)(2,1)}, u32[]{:S(2)}) copy-start(bf16[1,4096,128]{2,1,0:T(8,128)(2,1)} %param.28) | copy-start | bytes 3145732
  109.4 9.8 %copy-start.10 = (f32[128,8]{0,1:T(8,128)S(1)}, f32[128,8]{0,1:T(8,128)}, u32[]{:S(2)}) copy-start(f32[128,8]{0,1:T(8,128)} %param.26) | copy-start | bytes 12292
  110.8 26.0 %all-to-all-start.4 = ((bf16[512,2,128]{2,1,0:T(2,128)(2,1)}), bf16[512,2,128]{2,1,0:T(2,128)(2,1)S(1)}, u32[]{:S(2)}, u32[]{:S(2)}) async-start(bf16[512,2,128]{2,1,0:T(2,128)(2,1)} %reshape.642), calls=%async_computation.4 | async-start | bytes 524288 | tf_op jit(solution)/shard_map/all_to_all | solution.py:13

commit v7 on v6

--- a/solution.py
+++ b/solution.py
@@ -135,8 +135,8 @@
         out_weight.reshape(own_heads * HD, owners, columns),
         preferred_element_type=jnp.float32,
     )
-    got_proj = spread_to_owners(proj_blocks.astype(jnp.bfloat16), "expert")
-    projected_cols = jnp.sum(got_proj.astype(jnp.float32), axis=0)
+    got_proj = spread_to_owners(proj_blocks, "expert")
+    projected_cols = jnp.sum(got_proj, axis=0)
     attn_cols = projected_cols.astype(jnp.bfloat16)
     residual_cols = lax.dynamic_slice_in_dim(residual, owner_index * columns, columns, 1)
     stream_cols = residual_cols.astype(jnp.float32) + projected_cols

time: 139 us -> 145 us (1.043)
  waiting for transfers between devices: 41.6 us -> 45.7 us
    all_to_all x4, waiting for transfers between devices: 41.6 us -> 45.7 us  [spread_to_owners(): return lax.all_to_all(blocks, axis, 0, 0, tiled=True)]
    unnamed x39 -> x35, local copies, waits for them, and re-layouts: 6.08 us -> 7.98 us
  transfers between devices with their start and end apart: 4 -> 4, of which waited for: 4 -> 4; matrix products, arithmetic and copies ran while one was open for 8% -> 6% of each run, Pallas kernels for 0% -> 0%
where the time goes in v7:
time: 145 us; the launch traced here: 144 us
  waiting for transfers between devices  45.7 us (32%)
  starting transfers between devices  36.8 us (25%)
  blocking collectives  26.6 us (18%)
  local copies, waits for them, and re-layouts  19.6 us (14%)
  other arithmetic  9.89 us (7%)
  matrix products  4.55 us (3%)
    all_to_all x4, waiting for transfers between devices, spread_to_owners(): return lax.all_to_all(blocks, axis, 0, 0, tiled=True)  45.7 us
    all_to_all x4, starting transfers between devices, spread_to_owners(): return lax.all_to_all(blocks, axis, 0, 0, tiled=True)  36.8 us
    all_to_all x1, blocking collectives, spread_to_owners(): return lax.all_to_all(blocks, axis, 0, 0, tiled=True)  26.6 us
    unnamed x35, local copies, waits for them, and re-layouts  7.98 us
  transfers between devices with their start and end apart: 4, of which 4 were waited for; matrix products, arithmetic and copies ran while one was open for 6% of the time, Pallas kernels for 0%

profile of v7, /device:TPU:1, one launch (start us, length us, event | category | flops | bytes accessed | tf_op | source)
XLA Modules:
  0.0 144.2 jit_solution(17427995324502306415)
XLA Ops:
  0.7 1.1 copy.160
  2.5 0.8 reshape.504
  3.3 11.0 %all-to-all-start = ((bf16[8,8,2048]{2,1,0:T(8,128)(2,1)}), bf16[8,8,2048]{2,1,0:T(8,128)(2,1)S(1)}, u32[]{:S(2)}, u32[]{:S(2)}) async-start(bf16[8,8,2048]{2,1,0:T(8,128)(2,1)} %reshape.504), calls=%async_computation | async-start | bytes 524288 | tf_op jit(solution)/shard_map/all_to_all | solution.py:13
  17.4 1.6 %copy.106 = bf16[128,4096]{0,1:T(8,128)(2,1)S(1)} copy(bf16[128,4096]{1,0:T(8,128)(2,1)} %param.23) | data formatting | bytes 2097152 | tf_op args[7]
  19.2 5.4 %all-to-all-done = bf16[8,8,2048]{2,1,0:T(8,128)(2,1)S(1)} async-done(((bf16[8,8,2048]{2,1,0:T(8,128)(2,1)}), bf16[8,8,2048]{2,1,0:T(8,128)(2,1)S(1)}, u32[]{:S(2)}, u32[]{:S(2)}) %all-to-all-start) | async-done | bytes 262176 | tf_op jit(solution)/shard_map/all_to_all | solution.py:13
  28.6 1.0 reshape.636
  29.6 12.6 %all-to-all-start.1 = ((bf16[64,2,1088]{2,1,0:T(2,128)(2,1)}), bf16[64,2,1088]{2,1,0:T(2,128)(2,1)S(1)}, u32[]{:S(2)}, u32[]{:S(2)}) async-start(bf16[64,2,1088]{2,1,0:T(2,128)(2,1)} %reshape.636), calls=%async_computation.1 | async-start | bytes 589824 | tf_op jit(solution)/shard_map/all_to_all | solution.py:13
  42.2 2.7 %add_reduce_fusion = s32[128,64]{1,0:T(8,128)S(1)} fusion(s32[128]{0:T(128)S(1)} %eq.62), kind=kOutput, calls=%fused_computation.7 | output fusion | flops 1064960 | bytes 33280 | tf_op jit(solution)/shard_map/jit(cumsum)/reduce_window_sum | solution.py:152
  45.0 10.9 %all-to-all-done.1 = bf16[64,2,1088]{2,1,0:T(2,128)(2,1)S(1)} async-done(((bf16[64,2,1088]{2,1,0:T(2,128)(2,1)}), bf16[64,2,1088]{2,1,0:T(2,128)(2,1)S(1)}, u32[]{:S(2)}, u32[]{:S(2)}) %all-to-all-start.1) | async-done | bytes 278560 | tf_op jit(solution)/shard_map/all_to_all | solution.py:13
  56.3 1.2 copy.103
  58.7 1.4 fusion.12
  60.1 0.9 convolution_bitcast_fusion
  61.0 1.0 reshape.638
  62.1 4.8 %all-to-all-start.2 = ((f32[64,1,1024]{2,1,0:T(1,128)}), f32[64,1,1024]{2,1,0:T(1,128)S(1)}, u32[]{:S(2)}, u32[]{:S(2)}) async-start(f32[64,1,1024]{2,1,0:T(1,128)} %reshape.638), calls=%async_computation.2 | async-start | bytes 524288 | tf_op jit(solution)/shard_map/all_to_all | solution.py:13
  67.3 12.8 %all-to-all-done.2 = f32[64,1,1024]{2,1,0:T(1,128)S(1)} async-done(((f32[64,1,1024]{2,1,0:T(1,128)}), f32[64,1,1024]{2,1,0:T(1,128)S(1)}, u32[]{:S(2)}, u32[]{:S(2)}) %all-to-all-start.2) | async-done | bytes 262176 | tf_op jit(solution)/shard_map/all_to_all | solution.py:13
  80.6 1.3 reduce.11
  82.1 0.8 convert_add_fusion
  82.8 0.9 gather_fusion.4
  84.2 26.6 %all_to_all.25 = bf16[512,2,128]{2,1,0:T(2,128)(2,1)S(1)} all-to-all(bf16[512,2,128]{2,1,0:T(2,128)(2,1)S(1)} %reshape.640), channel_id=1, replica_groups=mesh['dp'=8,'expert'=64] {'dp','expert'}, dimensions={0} | all-to-all | bytes 524288 | tf_op jit(solution)/shard_map/all_to_all | solution.py:13
  112.9 1.5 %fusion.10 = f32[32,128]{1,0:T(8,128)S(1)} fusion(bf16[32,4096]{1,0:T(8,128)(2,1)S(1)} %convert_element_type.146, bf16[1,4096,128]{2,1,0:T(8,128)(2,1)} %param.27), kind=kOutput, calls=%fused_computation.24 | convolution fusion | flops 33554432 | bytes 1327104 | tf_op jit(solution)/shard_map/dot_general | solution.py:172
  116.0 0.9 reshape.642
  116.9 8.4 %all-to-all-start.4 = ((bf16[512,2,128]{2,1,0:T(2,128)(2,1)}), bf16[512,2,128]{2,1,0:T(2,128)(2,1)S(1)}, u32[]{:S(2)}, u32[]{:S(2)}) async-start(bf16[512,2,128]{2,1,0:T(2,128)(2,1)} %reshape.642), calls=%async_computation.4 | async-start | bytes 524288 | tf_op jit(solution)/shard_map/all_to_all | solution.py:13
  126.2 16.7 %all-to-all-done.4 = bf16[512,2,128]{2,1,0:T(2,128)(2,1)S(1)} async-done(((bf16[512,2,128]{2,1,0:T(2,128)(2,1)}), bf16[512,2,128]{2,1,0:T(2,128)(2,1)S(1)}, u32[]{:S(2)}, u32[]{:S(2)}) %all-to-all-start.4) | async-done | bytes 262176 | tf_op jit(solution)/shard_map/all_to_all | solution.py:13
  143.4 0.8 fusion.6
  (104 shorter events, 16.0 us)
Async XLA Ops:
  0.6 113.8 %copy-start = (bf16[1,128,4096]{2,1,0:T(8,128)(2,1)S(1)}, bf16[1,128,4096]{2,1,0:T(8,128)(2,1)}, u32[]{:S(2)}) copy-start(bf16[1,128,4096]{2,1,0:T(8,128)(2,1)} %param.29) | copy-start | bytes 3145732
  0.6 1.2 copy-start.9
  1.8 12.5 %copy-start.1 = (s32[64]{0:T(128)S(1)}, s32[64]{0:T(128)}, u32[]{:S(2)}) copy-start(s32[64]{0:T(128)} %param.22) | copy-start | bytes 772
  1.9 13.1 %copy-start.2 = (s32[64]{0:T(128)S(1)}, s32[64]{0:T(128)}, u32[]{:S(2)}) copy-start(s32[64]{0:T(128)} %param.21) | copy-start | bytes 772
  2.5 13.2 %copy-start.6 = (bf16[16,1024]{1,0:T(8,128)(2,1)S(1)}, bf16[16,1024]{1,0:T(8,128)(2,1)}, u32[]{:S(2)}) copy-start(bf16[16,1024]{1,0:T(8,128)(2,1)} %param.17) | copy-start | bytes 98308
  2.5 13.2 %copy-start.7 = (s32[128,8]{0,1:T(8,128)S(1)}, s32[128,8]{0,1:T(8,128)}, u32[]{:S(2)}) copy-start(s32[128,8]{0,1:T(8,128)} %param.25) | copy-start | bytes 12292
  3.3 12.5 %copy-start.4 = (bf16[16,8192]{1,0:T(8,128)(2,1)S(1)}, bf16[16,8192]{1,0:T(8,128)(2,1)}, u32[]{:S(2)}) copy-start(bf16[16,8192]{1,0:T(8,128)(2,1)} %param.16) | copy-start | bytes 786436
  3.3 21.4 %all-to-all-start = ((bf16[8,8,2048]{2,1,0:T(8,128)(2,1)}), bf16[8,8,2048]{2,1,0:T(8,128)(2,1)S(1)}, u32[]{:S(2)}, u32[]{:S(2)}) async-start(bf16[8,8,2048]{2,1,0:T(8,128)(2,1)} %reshape.504), calls=%async_computation | async-start | bytes 524288 | tf_op jit(solution)/shard_map/all_to_all | solution.py:13
  17.4 1.6 %copy-start.10 = (s32[16]{0:T(128)S(1)}, s32[16]{0:T(128)}, u32[]{:S(2)}) copy-start(s32[16]{0:T(128)} %param.19) | copy-start | bytes 196
  24.8 1.0 copy-start.5
  29.6 26.3 %all-to-all-start.1 = ((bf16[64,2,1088]{2,1,0:T(2,128)(2,1)}), bf16[64,2,1088]{2,1,0:T(2,128)(2,1)S(1)}, u32[]{:S(2)}, u32[]{:S(2)}) async-start(bf16[64,2,1088]{2,1,0:T(2,128)(2,1)} %reshape.636), calls=%async_computation.1 | async-start | bytes 589824 | tf_op jit(solution)/shard_map/all_to_all | solution.py:13
  62.1 18.0 %all-to-all-start.2 = ((f32[64,1,1024]{2,1,0:T(1,128)}), f32[64,1,1024]{2,1,0:T(1,128)S(1)}, u32[]{:S(2)}, u32[]{:S(2)}) async-start(f32[64,1,1024]{2,1,0:T(1,128)} %reshape.638), calls=%async_computation.2 | async-start | bytes 524288 | tf_op jit(solution)/shard_map/all_to_all | solution.py:13
  112.4 2.0 %copy-start.3 = (bf16[1,4096,128]{2,1,0:T(8,128)(2,1)S(1)}, bf16[1,4096,128]{2,1,0:T(8,128)(2,1)}, u32[]{:S(2)}) copy-start(bf16[1,4096,128]{2,1,0:T(8,128)(2,1)} %param.28) | copy-start | bytes 3145732
  115.5 9.8 %copy-start.8 = (f32[128,8]{0,1:T(8,128)S(1)}, f32[128,8]{0,1:T(8,128)}, u32[]{:S(2)}) copy-start(f32[128,8]{0,1:T(8,128)} %param.26) | copy-start | bytes 12292
  116.9 26.0 %all-to-all-start.4 = ((bf16[512,2,128]{2,1,0:T(2,128)(2,1)}), bf16[512,2,128]{2,1,0:T(2,128)(2,1)S(1)}, u32[]{:S(2)}, u32[]{:S(2)}) async-start(bf16[512,2,128]{2,1,0:T(2,128)(2,1)} %reshape.642), calls=%async_computation.4 | async-start | bytes 524288 | tf_op jit(solution)/shard_map/all_to_all | solution.py:13

commit v8 on v3

--- a/solution.py
+++ b/solution.py
@@ -55,36 +55,42 @@
         - group_index * local_rows
     )
     out_blocks = lax.dynamic_slice_in_dim(fork_block, group_index * groups, groups)
-    send_rows = jnp.where(
-        (owner_index >= out_blocks)[:, None, None],
-        kv_cache[outgoing],
-        jnp.zeros((), kv_cache.dtype),
-    )
+    send_rows = kv_cache[outgoing]
     arrived = lax.all_to_all(send_rows, "dp", split_axis=0, concat_axis=0, tiled=True)
     incoming = jnp.arange(groups, dtype=jnp.int32) * groups + group_index
     targets = fork_child[incoming] - group_index * local_rows
     take_new = owner_index >= fork_block[incoming]
-    cache = kv_cache.at[targets].set(jnp.where(take_new[:, None, None], arrived, kv_cache[targets]))
+    child_cache = jnp.where(take_new[:, None, None], arrived, kv_cache[targets])
 
     score_scale = 1.0 / math.sqrt(HD)
     positions = owner_index * positions_dev + jnp.arange(positions_dev, dtype=jnp.int32)
-    visible = positions[None, :] < lengths[:, None]
-    cached_keys = cache[:, :, :key_width].reshape(local_rows, positions_dev, KVH, HD)
-    cached_values = cache[:, :, key_width:].reshape(local_rows, positions_dev, KVH, HD)
-    grouped = query.reshape(local_rows, KVH, grouping, HD)
-    scores = (
-        jnp.einsum("bkgd,bpkd->bkgp", grouped, cached_keys, preferred_element_type=jnp.float32)
-        * score_scale
-    )
-    scores = jnp.where(visible[:, None, None, :], scores, -1e30)
-    highest = jnp.max(scores, axis=3)
-    weights = jnp.where(visible[:, None, None, :], jnp.exp(scores - highest[..., None]), 0.0)
-    weight_sum = jnp.sum(weights, axis=3)
-    partial_out = jnp.einsum(
-        "bkgp,bpkd->bkgd",
-        weights.astype(jnp.bfloat16),
-        cached_values,
-        preferred_element_type=jnp.float32,
+
+    def partial_attention(rows, cache_rows, row_lengths):
+        count = rows.shape[0]
+        visible = positions[None, :] < row_lengths[:, None]
+        cached_keys = cache_rows[:, :, :key_width].reshape(count, positions_dev, KVH, HD)
+        cached_values = cache_rows[:, :, key_width:].reshape(count, positions_dev, KVH, HD)
+        grouped = rows.reshape(count, KVH, grouping, HD)
+        scores = (
+            jnp.einsum("bkgd,bpkd->bkgp", grouped, cached_keys, preferred_element_type=jnp.float32)
+            * score_scale
+        )
+        scores = jnp.where(visible[:, None, None, :], scores, -1e30)
+        highest = jnp.max(scores, axis=3)
+        weights = jnp.where(visible[:, None, None, :], jnp.exp(scores - highest[..., None]), 0.0)
+        weight_sum = jnp.sum(weights, axis=3)
+        partial_out = jnp.einsum(
+            "bkgp,bpkd->bkgd",
+            weights.astype(jnp.bfloat16),
+            cached_values,
+            preferred_element_type=jnp.float32,
+        )
+        return partial_out, highest, weight_sum
+
+    before_fork = partial_attention(query, kv_cache, lengths)
+    of_children = partial_attention(query[targets], child_cache, lengths[targets])
+    partial_out, highest, weight_sum = (
+        whole.at[targets].set(child) for whole, child in zip(before_fork, of_children)
     )
 
     head_block = local_rows * own_heads

time: 138 us -> 140 us (1.014)
  waiting for transfers between devices: 41.4 us -> 43.4 us
  other arithmetic: 10.3 us -> 8.46 us
    all_to_all x3, waiting for transfers between devices: 36.9 us -> 40.6 us  [spread_to_owners(): return lax.all_to_all(blocks, axis, 0, 0, tiled=True)]
    gather x2 -> x4, local copies, waits for them, and re-layouts: 1.13 us -> 4.14 us  [the longest x1 2.31 us: shards(): send_rows = kv_cache[outgoing]]
    all_to_all x1, waiting for transfers between devices: 4.48 us -> 2.75 us  [shards(): lax.all_to_all(send_rows, 'dp', split_axis=0, concat_axis=0, tiled=True)]
    scatter x1 -> x3, local copies, waits for them, and re-layouts: 0.75 us -> 2.21 us  [shards(): whole.at[targets].set(child)]
    unnamed x39 -> x31, local copies, waits for them, and re-layouts: 4.8 us -> 4.64 us
  transfers between devices with their start and end apart: 4 -> 4, of which waited for: 4 -> 4; matrix products, arithmetic and copies ran while one was open for 9% -> 8% of each run, Pallas kernels for 0% -> 0%
where the time goes in v8:
time: 140 us; the launch traced here: 139 us
  waiting for transfers between devices  43.4 us (31%)
  starting transfers between devices  37.4 us (27%)
  blocking collectives  26.7 us (19%)
  local copies, waits for them, and re-layouts  16.9 us (12%)
  other arithmetic  8.46 us (6%)
  matrix products  4.99 us (4%)
    all_to_all x3, waiting for transfers between devices, spread_to_owners(): return lax.all_to_all(blocks, axis, 0, 0, tiled=True)  40.6 us
    all_to_all x1, blocking collectives, spread_to_owners(): return lax.all_to_all(blocks, axis, 0, 0, tiled=True)  26.7 us
    all_to_all x3, starting transfers between devices, spread_to_owners(): return lax.all_to_all(blocks, axis, 0, 0, tiled=True)  26.5 us
    all_to_all x1, starting transfers between devices, shards(): lax.all_to_all(send_rows, 'dp', split_axis=0, concat_axis=0, tiled=True)  10.9 us
    unnamed x31, local copies, waits for them, and re-layouts  4.64 us
  transfers between devices with their start and end apart: 4, of which 4 were waited for; matrix products, arithmetic and copies ran while one was open for 8% of the time, Pallas kernels for 0%

profile of v8, /device:TPU:1, one launch (start us, length us, event | category | flops | bytes accessed | tf_op | source)
XLA Modules:
  0.0 139.1 jit_solution(14463044026623159748)
XLA Ops:
  0.7 0.8 compare_select_fusion.1
  1.5 2.3 %gather_fusion.4 = bf16[8,16,1024]{2,1,0:T(8,128)(2,1)} fusion(bf16[16,16,1024]{2,1,0:T(8,128)(2,1)} %param.18, s32[1024]{0:T(1024)S(1)} %pad_clamp_fusion.1), kind=kCustom, calls=%fused_computation.4 | custom fusion | bytes 524320 | tf_op jit(solution)/shard_map/gather | solution.py:58
  3.8 10.9 %all-to-all-start = ((bf16[8,16,1024]{2,1,0:T(8,128)(2,1)}), bf16[8,16,1024]{2,1,0:T(8,128)(2,1)S(1)}, u32[]{:S(2)}, u32[]{:S(2)}) async-start(bf16[8,16,1024]{2,1,0:T(8,128)(2,1)} %gather_fusion.4), calls=%async_computation | async-start | bytes 524288 | tf_op jit(solution)/shard_map/all_to_all | solution.py:59
  17.9 2.7 %add_reduce_fusion = s32[128,64]{1,0:T(8,128)S(1)} fusion(s32[128]{0:T(128)S(1)} %eq.62), kind=kOutput, calls=%fused_computation.11 | output fusion | flops 1064960 | bytes 33280 | tf_op jit(solution)/shard_map/jit(cumsum)/reduce_window_sum | solution.py:164
  22.3 2.8 %all-to-all-done = bf16[8,16,1024]{2,1,0:T(8,128)(2,1)S(1)} async-done(((bf16[8,16,1024]{2,1,0:T(8,128)(2,1)}), bf16[8,16,1024]{2,1,0:T(8,128)(2,1)S(1)}, u32[]{:S(2)}, u32[]{:S(2)}) %all-to-all-start) | async-done | bytes 262176 | tf_op jit(solution)/shard_map/all_to_all | solution.py:59
  25.9 0.8 scatter_fusion
  26.7 0.7 scatter_fusion.1
  27.5 0.7 scatter_fusion.2
  28.7 0.8 pad_maximum_fusion
  29.5 12.6 %all-to-all-start.1 = ((bf16[64,17,128]{2,1,0:T(8,128)(2,1)}), bf16[64,17,128]{2,1,0:T(8,128)(2,1)S(1)}, u32[]{:S(2)}, u32[]{:S(2)}) async-start(bf16[64,17,128]{2,1,0:T(8,128)(2,1)} %pad_maximum_fusion), calls=%async_computation.1 | async-start | bytes 786432 | tf_op jit(solution)/shard_map/all_to_all | solution.py:13
  42.2 1.6 %copy.124 = bf16[128,4096]{0,1:T(8,128)(2,1)S(1)} copy(bf16[128,4096]{1,0:T(8,128)(2,1)} %param.23) | data formatting | bytes 2097152 | tf_op args[7]
  44.0 13.1 %all-to-all-done.1 = bf16[64,17,128]{2,1,0:T(8,128)(2,1)S(1)} async-done(((bf16[64,17,128]{2,1,0:T(8,128)(2,1)}), bf16[64,17,128]{2,1,0:T(8,128)(2,1)S(1)}, u32[]{:S(2)}, u32[]{:S(2)}) %all-to-all-start.1) | async-done | bytes 278560 | tf_op jit(solution)/shard_map/all_to_all | solution.py:13
  58.0 0.9 fusion.4
  58.9 0.9 reshape.698
  59.8 5.6 %all-to-all-start.2 = ((bf16[64,2,512]{2,1,0:T(2,128)(2,1)}), bf16[64,2,512]{2,1,0:T(2,128)(2,1)S(1)}, u32[]{:S(2)}, u32[]{:S(2)}) async-start(bf16[64,2,512]{2,1,0:T(2,128)(2,1)} %reshape.698), calls=%async_computation.2 | async-start | bytes 262144 | tf_op jit(solution)/shard_map/all_to_all | solution.py:13
  65.6 10.9 %all-to-all-done.2 = bf16[64,2,512]{2,1,0:T(2,128)(2,1)S(1)} async-done(((bf16[64,2,512]{2,1,0:T(2,128)(2,1)}), bf16[64,2,512]{2,1,0:T(2,128)(2,1)S(1)}, u32[]{:S(2)}, u32[]{:S(2)}) %all-to-all-start.2) | async-done | bytes 131104 | tf_op jit(solution)/shard_map/all_to_all | solution.py:13
  76.8 0.8 convert_add_fusion
  77.6 0.9 gather_fusion.6
  79.0 26.7 %all_to_all.25 = bf16[512,2,128]{2,1,0:T(2,128)(2,1)S(1)} all-to-all(bf16[512,2,128]{2,1,0:T(2,128)(2,1)S(1)} %reshape.700), channel_id=1, replica_groups=mesh['dp'=8,'expert'=64] {'dp','expert'}, dimensions={0} | all-to-all | bytes 524288 | tf_op jit(solution)/shard_map/all_to_all | solution.py:13
  107.8 1.5 %fusion.11 = f32[32,128]{1,0:T(8,128)S(1)} fusion(bf16[32,4096]{1,0:T(8,128)(2,1)S(1)} %convert_element_type.162, bf16[1,4096,128]{2,1,0:T(8,128)(2,1)} %param.27), kind=kOutput, calls=%fused_computation.29 | convolution fusion | flops 33554432 | bytes 1327104 | tf_op jit(solution)/shard_map/dot_general | solution.py:184
  110.8 0.9 reshape.702
  111.8 8.4 %all-to-all-start.4 = ((bf16[512,2,128]{2,1,0:T(2,128)(2,1)}), bf16[512,2,128]{2,1,0:T(2,128)(2,1)S(1)}, u32[]{:S(2)}, u32[]{:S(2)}) async-start(bf16[512,2,128]{2,1,0:T(2,128)(2,1)} %reshape.702), calls=%async_computation.4 | async-start | bytes 524288 | tf_op jit(solution)/shard_map/all_to_all | solution.py:13
  121.1 16.7 %all-to-all-done.4 = bf16[512,2,128]{2,1,0:T(2,128)(2,1)S(1)} async-done(((bf16[512,2,128]{2,1,0:T(2,128)(2,1)}), bf16[512,2,128]{2,1,0:T(2,128)(2,1)S(1)}, u32[]{:S(2)}, u32[]{:S(2)}) %all-to-all-start.4) | async-done | bytes 262176 | tf_op jit(solution)/shard_map/all_to_all | solution.py:13
  138.3 0.8 fusion.7
  (106 shorter events, 13.2 us)
Async XLA Ops:
  0.6 108.7 %copy-start = (bf16[1,128,4096]{2,1,0:T(8,128)(2,1)S(1)}, bf16[1,128,4096]{2,1,0:T(8,128)(2,1)}, u32[]{:S(2)}) copy-start(bf16[1,128,4096]{2,1,0:T(8,128)(2,1)} %param.29) | copy-start | bytes 3145732
  0.6 14.4 %copy-start.5 = (bf16[16,16,1024]{2,1,0:T(8,128)(2,1)S(1)}, bf16[16,16,1024]{2,1,0:T(8,128)(2,1)}, u32[]{:S(2)}) copy-start(bf16[16,16,1024]{2,1,0:T(8,128)(2,1)} %param.18) | copy-start | bytes 1572868
  0.7 14.1 %copy-start.8 = (s32[128,8]{0,1:T(8,128)S(1)}, s32[128,8]{0,1:T(8,128)}, u32[]{:S(2)}) copy-start(s32[128,8]{0,1:T(8,128)} %param.25) | copy-start | bytes 12292
  1.5 13.6 %copy-start.2 = (s32[64]{0:T(128)S(1)}, s32[64]{0:T(128)}, u32[]{:S(2)}) copy-start(s32[64]{0:T(128)} %param.21) | copy-start | bytes 772
  3.8 21.2 %all-to-all-start = ((bf16[8,16,1024]{2,1,0:T(8,128)(2,1)}), bf16[8,16,1024]{2,1,0:T(8,128)(2,1)S(1)}, u32[]{:S(2)}, u32[]{:S(2)}) async-start(bf16[8,16,1024]{2,1,0:T(8,128)(2,1)} %gather_fusion.4), calls=%async_computation | async-start | bytes 524288 | tf_op jit(solution)/shard_map/all_to_all | solution.py:59
  15.1 1.4 copy-start.1
  15.1 2.0 %copy-start.3 = (s32[64]{0:T(128)S(1)}, s32[64]{0:T(128)}, u32[]{:S(2)}) copy-start(s32[64]{0:T(128)} %param.22) | copy-start | bytes 772
  15.2 2.7 %copy-start.7 = (bf16[16,1024]{1,0:T(8,128)(2,1)S(1)}, bf16[16,1024]{1,0:T(8,128)(2,1)}, u32[]{:S(2)}) copy-start(bf16[16,1024]{1,0:T(8,128)(2,1)} %param.17) | copy-start | bytes 98308
  15.2 5.4 %copy-start.4 = (bf16[16,8192]{1,0:T(8,128)(2,1)S(1)}, bf16[16,8192]{1,0:T(8,128)(2,1)}, u32[]{:S(2)}) copy-start(bf16[16,8192]{1,0:T(8,128)(2,1)} %param.16) | copy-start | bytes 786436
  29.5 27.6 %all-to-all-start.1 = ((bf16[64,17,128]{2,1,0:T(8,128)(2,1)}), bf16[64,17,128]{2,1,0:T(8,128)(2,1)S(1)}, u32[]{:S(2)}, u32[]{:S(2)}) async-start(bf16[64,17,128]{2,1,0:T(8,128)(2,1)} %pad_maximum_fusion), calls=%async_computation.1 | async-start | bytes 786432 | tf_op jit(solution)/shard_map/all_to_all | solution.py:13
  59.8 16.7 %all-to-all-start.2 = ((bf16[64,2,512]{2,1,0:T(2,128)(2,1)}), bf16[64,2,512]{2,1,0:T(2,128)(2,1)S(1)}, u32[]{:S(2)}, u32[]{:S(2)}) async-start(bf16[64,2,512]{2,1,0:T(2,128)(2,1)} %reshape.698), calls=%async_computation.2 | async-start | bytes 262144 | tf_op jit(solution)/shard_map/all_to_all | solution.py:13
  107.3 2.0 %copy-start.6 = (bf16[1,4096,128]{2,1,0:T(8,128)(2,1)S(1)}, bf16[1,4096,128]{2,1,0:T(8,128)(2,1)}, u32[]{:S(2)}) copy-start(bf16[1,4096,128]{2,1,0:T(8,128)(2,1)} %param.28) | copy-start | bytes 3145732
  110.4 9.8 %copy-start.9 = (f32[128,8]{0,1:T(8,128)S(1)}, f32[128,8]{0,1:T(8,128)}, u32[]{:S(2)}) copy-start(f32[128,8]{0,1:T(8,128)} %param.26) | copy-start | bytes 12292
  111.8 26.0 %all-to-all-start.4 = ((bf16[512,2,128]{2,1,0:T(2,128)(2,1)}), bf16[512,2,128]{2,1,0:T(2,128)(2,1)S(1)}, u32[]{:S(2)}, u32[]{:S(2)}) async-start(bf16[512,2,128]{2,1,0:T(2,128)(2,1)} %reshape.702), calls=%async_computation.4 | async-start | bytes 524288 | tf_op jit(solution)/shard_map/all_to_all | solution.py:13

commit v9 on v3

--- a/solution.py
+++ b/solution.py
@@ -183,11 +183,13 @@
     out_blocks = outputs.astype(jnp.bfloat16).reshape(groups, capacity, owners, columns)
     out_blocks = out_blocks.transpose(0, 2, 1, 3).reshape(groups * owners, capacity, columns)
     partials = spread_to_owners(out_blocks, ("dp", "expert"))
-    partials = partials.reshape(groups, experts_total, capacity, columns)
-    summed = jnp.sum(partials.astype(jnp.float32), axis=0)
-    mix_cols = jnp.einsum(
-        "tes,esc->tc", slot_weight, summed, precision=lax.Precision.HIGHEST
-    ).astype(jnp.bfloat16)
+    partials = partials.reshape(groups * experts_total * capacity, columns)
+    shard_weight = jnp.broadcast_to(
+        slot_weight.astype(jnp.bfloat16)[:, None], (local_rows, groups) + slot_weight.shape[1:]
+    ).reshape(local_rows, groups * experts_total * capacity)
+    mix_cols = jnp.dot(shard_weight, partials, preferred_element_type=jnp.float32).astype(
+        jnp.bfloat16
+    )
     return (attn_cols, mix_cols)
 
 

time: 138 us -> 139 us (level)
  waiting for transfers between devices: 41.4 us -> 44.2 us
  other arithmetic: 10.3 us -> 8.73 us
    all_to_all x3, waiting for transfers between devices: 36.9 us -> 41.5 us  [spread_to_owners(): return lax.all_to_all(blocks, axis, 0, 0, tiled=True)]
    unnamed x39 -> x33, local copies, waits for them, and re-layouts: 4.8 us -> 7.34 us
    all_to_all x1, waiting for transfers between devices: 4.48 us -> 2.68 us  [shards(): lax.all_to_all(send_rows, 'dp', split_axis=0, concat_axis=0, tiled=True)]
  transfers between devices with their start and end apart: 4 -> 4, of which waited for: 4 -> 4; matrix products, arithmetic and copies ran while one was open for 9% -> 7% of each run, Pallas kernels for 0% -> 0%
where the time goes in v9:
time: 139 us; the launch traced here: 138 us
  waiting for transfers between devices  44.2 us (32%)
  starting transfers between devices  37.4 us (27%)
  blocking collectives  26.5 us (19%)
  local copies, waits for them, and re-layouts  15.4 us (11%)
  other arithmetic  8.73 us (6%)
  matrix products  4.62 us (3%)
    all_to_all x3, waiting for transfers between devices, spread_to_owners(): return lax.all_to_all(blocks, axis, 0, 0, tiled=True)  41.5 us
    all_to_all x3, starting transfers between devices, spread_to_owners(): return lax.all_to_all(blocks, axis, 0, 0, tiled=True)  26.6 us
    all_to_all x1, blocking collectives, spread_to_owners(): return lax.all_to_all(blocks, axis, 0, 0, tiled=True)  26.5 us
    all_to_all x1, starting transfers between devices, shards(): lax.all_to_all(send_rows, 'dp', split_axis=0, concat_axis=0, tiled=True)  10.9 us
    unnamed x33, local copies, waits for them, and re-layouts  7.34 us
  transfers between devices with their start and end apart: 4, of which 4 were waited for; matrix products, arithmetic and copies ran while one was open for 7% of the time, Pallas kernels for 0%

profile of v9, /device:TPU:1, one launch (start us, length us, event | category | flops | bytes accessed | tf_op | source)
XLA Modules:
  0.0 138.1 jit_solution(16715880468244130084)
XLA Ops:
  0.7 1.1 copy.144
  2.6 0.8 broadcast_select_fusion
  3.3 10.9 %all-to-all-start = ((bf16[8,16,1024]{2,1,0:T(8,128)(2,1)}), bf16[8,16,1024]{2,1,0:T(8,128)(2,1)S(1)}, u32[]{:S(2)}, u32[]{:S(2)}) async-start(bf16[8,16,1024]{2,1,0:T(8,128)(2,1)} %broadcast_select_fusion), calls=%async_computation | async-start | bytes 524288 | tf_op jit(solution)/shard_map/all_to_all | solution.py:63
  15.3 2.7 %add_reduce_fusion = s32[128,64]{1,0:T(8,128)S(1)} fusion(s32[128]{0:T(128)S(1)} %eq.62), kind=kOutput, calls=%fused_computation.7 | output fusion | flops 1064960 | bytes 33280 | tf_op jit(solution)/shard_map/jit(cumsum)/reduce_window_sum | solution.py:158
  20.2 1.6 %copy.99 = bf16[128,4096]{0,1:T(8,128)(2,1)S(1)} copy(bf16[128,4096]{1,0:T(8,128)(2,1)} %param.23) | data formatting | bytes 2097152 | tf_op args[7]
  21.9 2.7 %all-to-all-done = bf16[8,16,1024]{2,1,0:T(8,128)(2,1)S(1)} async-done(((bf16[8,16,1024]{2,1,0:T(8,128)(2,1)}), bf16[8,16,1024]{2,1,0:T(8,128)(2,1)S(1)}, u32[]{:S(2)}, u32[]{:S(2)}) %all-to-all-start) | async-done | bytes 262176 | tf_op jit(solution)/shard_map/all_to_all | solution.py:63
  24.7 0.8 scatter_fusion
  25.5 0.9 copy-done.5
  27.9 0.8 pad_maximum_fusion
  28.7 12.6 %all-to-all-start.1 = ((bf16[64,17,128]{2,1,0:T(8,128)(2,1)}), bf16[64,17,128]{2,1,0:T(8,128)(2,1)S(1)}, u32[]{:S(2)}, u32[]{:S(2)}) async-start(bf16[64,17,128]{2,1,0:T(8,128)(2,1)} %pad_maximum_fusion), calls=%async_computation.1 | async-start | bytes 786432 | tf_op jit(solution)/shard_map/all_to_all | solution.py:13
  41.5 0.8 fusion.34
  42.3 14.0 %all-to-all-done.1 = bf16[64,17,128]{2,1,0:T(8,128)(2,1)S(1)} async-done(((bf16[64,17,128]{2,1,0:T(8,128)(2,1)}), bf16[64,17,128]{2,1,0:T(8,128)(2,1)S(1)}, u32[]{:S(2)}, u32[]{:S(2)}) %all-to-all-start.1) | async-done | bytes 278560 | tf_op jit(solution)/shard_map/all_to_all | solution.py:13
  57.2 0.9 fusion.5
  58.1 0.9 reshape.637
  59.0 5.6 %all-to-all-start.2 = ((bf16[64,2,512]{2,1,0:T(2,128)(2,1)}), bf16[64,2,512]{2,1,0:T(2,128)(2,1)S(1)}, u32[]{:S(2)}, u32[]{:S(2)}) async-start(bf16[64,2,512]{2,1,0:T(2,128)(2,1)} %reshape.637), calls=%async_computation.2 | async-start | bytes 262144 | tf_op jit(solution)/shard_map/all_to_all | solution.py:13
  64.7 11.0 %all-to-all-done.2 = bf16[64,2,512]{2,1,0:T(2,128)(2,1)S(1)} async-done(((bf16[64,2,512]{2,1,0:T(2,128)(2,1)}), bf16[64,2,512]{2,1,0:T(2,128)(2,1)S(1)}, u32[]{:S(2)}, u32[]{:S(2)}) %all-to-all-start.2) | async-done | bytes 131104 | tf_op jit(solution)/shard_map/all_to_all | solution.py:13
  76.0 0.8 convert_add_fusion
  76.8 0.9 gather_fusion.4
  78.2 26.5 %all_to_all.25 = bf16[512,2,128]{2,1,0:T(2,128)(2,1)S(1)} all-to-all(bf16[512,2,128]{2,1,0:T(2,128)(2,1)S(1)} %reshape.639), channel_id=1, replica_groups=mesh['dp'=8,'expert'=64] {'dp','expert'}, dimensions={0} | all-to-all | bytes 524288 | tf_op jit(solution)/shard_map/all_to_all | solution.py:13
  106.8 1.5 %fusion.10 = f32[32,128]{1,0:T(8,128)S(1)} fusion(bf16[32,4096]{1,0:T(8,128)(2,1)S(1)} %convert_element_type.160, bf16[1,4096,128]{2,1,0:T(8,128)(2,1)} %param.27), kind=kOutput, calls=%fused_computation.23 | convolution fusion | flops 33554432 | bytes 1327104 | tf_op jit(solution)/shard_map/dot_general | solution.py:178
  109.9 0.9 reshape.641
  110.8 8.4 %all-to-all-start.4 = ((bf16[512,2,128]{2,1,0:T(2,128)(2,1)}), bf16[512,2,128]{2,1,0:T(2,128)(2,1)S(1)}, u32[]{:S(2)}, u32[]{:S(2)}) async-start(bf16[512,2,128]{2,1,0:T(2,128)(2,1)} %reshape.641), calls=%async_computation.4 | async-start | bytes 524288 | tf_op jit(solution)/shard_map/all_to_all | solution.py:13
  120.3 16.5 %all-to-all-done.4 = bf16[512,2,128]{2,1,0:T(2,128)(2,1)S(1)} async-done(((bf16[512,2,128]{2,1,0:T(2,128)(2,1)}), bf16[512,2,128]{2,1,0:T(2,128)(2,1)S(1)}, u32[]{:S(2)}, u32[]{:S(2)}) %all-to-all-start.4) | async-done | bytes 262176 | tf_op jit(solution)/shard_map/all_to_all | solution.py:13
  137.2 0.9 convolution_convert_fusion.3
  (102 shorter events, 12.6 us)
Async XLA Ops:
  0.6 107.7 %copy-start = (bf16[1,128,4096]{2,1,0:T(8,128)(2,1)S(1)}, bf16[1,128,4096]{2,1,0:T(8,128)(2,1)}, u32[]{:S(2)}) copy-start(bf16[1,128,4096]{2,1,0:T(8,128)(2,1)} %param.29) | copy-start | bytes 3145732
  0.6 1.2 copy-start.9
  0.7 1.8 %copy-start.1 = (s32[64]{0:T(128)S(1)}, s32[64]{0:T(128)}, u32[]{:S(2)}) copy-start(s32[64]{0:T(128)} %param.22) | copy-start | bytes 772
  1.8 12.4 %copy-start.7 = (s32[128,8]{0,1:T(8,128)S(1)}, s32[128,8]{0,1:T(8,128)}, u32[]{:S(2)}) copy-start(s32[128,8]{0,1:T(8,128)} %param.25) | copy-start | bytes 12292
  1.8 12.8 %copy-start.2 = (s32[64]{0:T(128)S(1)}, s32[64]{0:T(128)}, u32[]{:S(2)}) copy-start(s32[64]{0:T(128)} %param.21) | copy-start | bytes 772
  1.9 13.4 %copy-start.6 = (bf16[16,1024]{1,0:T(8,128)(2,1)S(1)}, bf16[16,1024]{1,0:T(8,128)(2,1)}, u32[]{:S(2)}) copy-start(bf16[16,1024]{1,0:T(8,128)(2,1)} %param.17) | copy-start | bytes 98308
  3.3 21.2 %all-to-all-start = ((bf16[8,16,1024]{2,1,0:T(8,128)(2,1)}), bf16[8,16,1024]{2,1,0:T(8,128)(2,1)S(1)}, u32[]{:S(2)}, u32[]{:S(2)}) async-start(bf16[8,16,1024]{2,1,0:T(8,128)(2,1)} %broadcast_select_fusion), calls=%async_computation | async-start | bytes 524288 | tf_op jit(solution)/shard_map/all_to_all | solution.py:63
  14.2 5.2 %copy-start.4 = (bf16[16,8192]{1,0:T(8,128)(2,1)S(1)}, bf16[16,8192]{1,0:T(8,128)(2,1)}, u32[]{:S(2)}) copy-start(bf16[16,8192]{1,0:T(8,128)(2,1)} %param.16) | copy-start | bytes 786436
  20.2 1.7 %copy-start.10 = (s32[16]{0:T(128)S(1)}, s32[16]{0:T(128)}, u32[]{:S(2)}) copy-start(s32[16]{0:T(128)} %param.19) | copy-start | bytes 196
  25.4 1.0 copy-start.5
  28.7 27.6 %all-to-all-start.1 = ((bf16[64,17,128]{2,1,0:T(8,128)(2,1)}), bf16[64,17,128]{2,1,0:T(8,128)(2,1)S(1)}, u32[]{:S(2)}, u32[]{:S(2)}) async-start(bf16[64,17,128]{2,1,0:T(8,128)(2,1)} %pad_maximum_fusion), calls=%async_computation.1 | async-start | bytes 786432 | tf_op jit(solution)/shard_map/all_to_all | solution.py:13
  59.0 16.7 %all-to-all-start.2 = ((bf16[64,2,512]{2,1,0:T(2,128)(2,1)}), bf16[64,2,512]{2,1,0:T(2,128)(2,1)S(1)}, u32[]{:S(2)}, u32[]{:S(2)}) async-start(bf16[64,2,512]{2,1,0:T(2,128)(2,1)} %reshape.637), calls=%async_computation.2 | async-start | bytes 262144 | tf_op jit(solution)/shard_map/all_to_all | solution.py:13
  106.3 2.0 %copy-start.3 = (bf16[1,4096,128]{2,1,0:T(8,128)(2,1)S(1)}, bf16[1,4096,128]{2,1,0:T(8,128)(2,1)}, u32[]{:S(2)}) copy-start(bf16[1,4096,128]{2,1,0:T(8,128)(2,1)} %param.28) | copy-start | bytes 3145732
  109.4 9.8 %copy-start.8 = (f32[128,8]{0,1:T(8,128)S(1)}, f32[128,8]{0,1:T(8,128)}, u32[]{:S(2)}) copy-start(f32[128,8]{0,1:T(8,128)} %param.26) | copy-start | bytes 12292
  110.8 26.0 %all-to-all-start.4 = ((bf16[512,2,128]{2,1,0:T(2,128)(2,1)}), bf16[512,2,128]{2,1,0:T(2,128)(2,1)S(1)}, u32[]{:S(2)}, u32[]{:S(2)}) async-start(bf16[512,2,128]{2,1,0:T(2,128)(2,1)} %reshape.641), calls=%async_computation.4 | async-start | bytes 524288 | tf_op jit(solution)/shard_map/all_to_all | solution.py:13
